TPU v7x, 256 devices: a whole 4x4x8 slice. The times are simulated.
256 devices in a mesh: bond: 64 (over z, y, core), mpo: 4 (over x).
Axes of the slice: x: 4, y: 4, z: 8, core: 2. Of those that a mesh axis runs over, the one named last changes fastest.
Arguments:
- wave_blocks: bfloat16 [256, 8, 64, 256], P('bond'), may hold values from -6 to 6
- left_env: bfloat16 [256, 20, 4096], P('bond', 'mpo'), may hold values from -0.75 to 0.75
- right_env: bfloat16 [256, 20, 4096], P('bond', 'mpo'), may hold values from -0.75 to 0.75
- mpo_coef: float32 [20, 8], P('mpo'), may hold values from -3 to 3
- mpo_mask: int32 [20, 8], P('mpo'), may hold values 0 or 1
- right_sector: int32 [256, 8], replicated, may hold values from 0 to 255, as said below
Outputs:
- sigma_blocks: bfloat16 [256, 8, 64, 256], P('bond')
Inputs may be any that keep to these rules, and one draw needn't show every extreme that they name: `right_sector`: right sector b is held by bond device b // 4. The 32 blocks of the left sectors of one bond device (rows in order) name sectors of at most 1 block on any one bond device, and exactly 1 on some.
All inputs are finite; a program needn't handle non-finite values. No bound on the sum of `mpo_mask` on one device may be relied on, other than what follows from the above.
Results may differ from a plain program's by a relative error of at most 0.013.
Values may be sent and summed in bfloat16 or wider, within the bound.
No kernel may reach another device: no remote copies, remote signals or barrier semaphores. Data moves between devices by JAX's collectives and lax.ppermute only.
A program may use at most 128 MiB of HBM per device.

v0:
```python
import jax
import jax.numpy as jnp
from jax import lax
from jax.sharding import PartitionSpec as P


def apply_terms(wave_rows, left_rows, right_rows):
    slot_count, block_width, column_count = wave_rows.shape
    term_count = left_rows.shape[1]
    vectors = column_count // block_width
    summed = jnp.zeros((slot_count, block_width, vectors, block_width), jnp.float32)
    for term in range(term_count):
        left_term = left_rows[:, term].reshape(slot_count, block_width, block_width)
        sectioned = jnp.einsum(
            "plk,pkc->plc", left_term, wave_rows, preferred_element_type=jnp.float32
        ).astype(jnp.bfloat16)
        right_term = right_rows[:, term].reshape(slot_count, block_width, block_width)
        summed = summed + jnp.einsum(
            "plvr,psr->plvs",
            sectioned.reshape(slot_count, block_width, vectors, block_width),
            right_term,
            preferred_element_type=jnp.float32,
        )
    return summed.reshape(slot_count, block_width, column_count).astype(jnp.bfloat16)


def route_tables(destinations, bond_index, capacity, sec_local, bond_count):
    owner_ids = destinations // sec_local
    device_ids = jnp.arange(bond_count, dtype=jnp.int32)
    owner_hits = (owner_ids[:, :, None] == device_ids[None, None, :]).astype(jnp.int32)
    earlier = jnp.cumsum(owner_hits, axis=1) - owner_hits
    slot_rank = jnp.sum(earlier * owner_hits, axis=2)
    own_slots = lax.dynamic_index_in_dim(
        owner_ids * capacity + slot_rank, bond_index, 0, keepdims=False
    )
    incoming = owner_ids == bond_index
    slot_pick = (
        (slot_rank[:, :, None] == jnp.arange(capacity, dtype=jnp.int32)[None, None, :])
        & incoming[:, :, None]
    ).astype(jnp.float32)
    local_pick = (
        (destinations % sec_local)[:, :, None]
        == jnp.arange(sec_local, dtype=jnp.int32)[None, None, :]
    ).astype(jnp.float32)
    sector_table = jnp.einsum("skr,ski->sri", slot_pick, local_pick).reshape(
        bond_count * capacity, sec_local
    )
    return (own_slots, sector_table)


def per_device(wave_blocks, left_env, right_env, mpo_coef, mpo_mask, right_sector):
    sec_local, class_count, block_width, column_count = wave_blocks.shape
    term_local = left_env.shape[1]
    blocks_local = sec_local * class_count
    bond_count = lax.axis_size("bond")
    capacity = max(1, 2 * blocks_local // bond_count)
    bond_index = lax.axis_index("bond")
    term_gains = mpo_coef * mpo_mask.astype(jnp.float32)
    wave_rows = wave_blocks.reshape(blocks_local, block_width, column_count)
    destinations = right_sector.reshape(bond_count, blocks_local)
    own_slots, sector_table = route_tables(
        destinations, bond_index, capacity, sec_local, bond_count
    )
    slot_total = bond_count * capacity
    left_scaled = (
        left_env[:, None, :, :].astype(jnp.float32) * jnp.transpose(term_gains)[None, :, :, None]
    ).astype(jnp.bfloat16)
    left_scaled = left_scaled.reshape(blocks_local, term_local, block_width * block_width)
    send_wave = (
        jnp.zeros((slot_total, block_width, column_count), jnp.bfloat16)
        .at[own_slots]
        .set(wave_rows)
    )
    send_left = (
        jnp.zeros((slot_total, term_local, block_width * block_width), jnp.bfloat16)
        .at[own_slots]
        .set(left_scaled)
    )
    right_blocks = jnp.dot(
        sector_table.astype(jnp.bfloat16),
        right_env.reshape(sec_local, -1),
        preferred_element_type=jnp.float32,
    )
    right_blocks = right_blocks.astype(jnp.bfloat16).reshape(
        slot_total, term_local, block_width * block_width
    )
    got_wave, got_left = (
        lax.all_to_all(send_wave, "bond", split_axis=0, concat_axis=0, tiled=True),
        lax.all_to_all(send_left, "bond", split_axis=0, concat_axis=0, tiled=True),
    )
    partial_sum = apply_terms(got_wave, got_left, right_blocks)
    arrived = lax.all_to_all(partial_sum, "bond", split_axis=0, concat_axis=0, tiled=True)
    returned = arrived[own_slots]
    summed = lax.psum(returned.astype(jnp.float32).astype(jnp.bfloat16), "mpo")
    return summed.reshape(wave_blocks.shape)


def solution(mesh):
    return jax.shard_map(
        per_device,
        mesh=mesh,
        in_specs=(
            P("bond", None, None, None),
            P("bond", "mpo", None),
            P("bond", "mpo", None),
            P("mpo", None),
            P("mpo", None),
            P(),
        ),
        out_specs=P("bond", None, None, None),
        check_vma=False,
    )
```

profile of v0, /device:TPU:8, one launch (start us, length us, event | category | flops | bytes accessed | tf_op | source)
XLA Modules:
  0.0 430.4 jit_solution(16720247989495655707)
XLA Ops:
  6.5 0.0 copy-start
  6.5 0.9 copy.47
  7.4 0.1 reshape.125
  7.5 0.1 copy.48
  7.6 1.2 select_reduce_fusion
  8.8 0.2 fusion.25
  9.0 1.0 copy.52
  10.0 0.7 multiply_bitcast_fusion
  10.7 0.1 copy.53
  10.8 0.4 fusion
  11.2 2.5 broadcast_in_dim.4
  13.7 5.4 %scatter_fusion = bf16[64,5,4096]{2,1,0:T(8,128)(2,1)} fusion(bf16[64,5,4096]{2,1,0:T(8,128)(2,1)} %broadcast_in_dim.4, s32[32]{0:T(128)S(1)} %fusion.29, bf16[32,5,4096]{2,1,0:T(8,128)(2,1)S(1)} %fusion), kind=kCustom, calls=%fused_computation.1 | custom fusion | bytes 3932288 | tf_op jit(solution)/shard_map/scatter | solution.py:77
  19.1 12.4 %all-to-all-start = ((bf16[64,5,4096]{2,1,0:T(8,128)(2,1)}), bf16[64,5,4096]{2,1,0:T(8,128)(2,1)}, u32[]{:S(2)}, u32[]{:S(2)}) async-start(bf16[64,5,4096]{2,1,0:T(8,128)(2,1)} %scatter_fusion), calls=%async_computation | async-start | bytes 8388608 | tf_op jit(solution)/shard_map/all_to_all | solution.py:89
  31.5 0.2 broadcast_in_dim.5
  31.8 0.0 copy-done.11
  31.8 1.6 scatter_fusion.1
  33.4 0.0 copy-start.5
  33.4 1.3 copy-done.5
  34.8 92.9 %all-to-all-done = bf16[64,5,4096]{2,1,0:T(8,128)(2,1)} async-done(((bf16[64,5,4096]{2,1,0:T(8,128)(2,1)}), bf16[64,5,4096]{2,1,0:T(8,128)(2,1)}, u32[]{:S(2)}, u32[]{:S(2)}) %all-to-all-start) | async-done | bytes 2621472 | tf_op jit(solution)/shard_map/all_to_all | solution.py:89
  127.6 5.8 %all-to-all-start.1 = ((bf16[64,64,256]{2,1,0:T(8,128)(2,1)}), bf16[64,64,256]{2,1,0:T(8,128)(2,1)S(1)}, u32[]{:S(2)}, u32[]{:S(2)}) async-start(bf16[64,64,256]{2,1,0:T(8,128)(2,1)} %copy-done.5), calls=%async_computation.1 | async-start | bytes 4194304 | tf_op jit(solution)/shard_map/all_to_all | solution.py:88
  133.4 0.1 copy.61
  133.6 0.1 copy.54
  133.6 0.4 fusion.22
  134.1 2.4 convolution_convert_fusion
  136.5 6.6 %reshape.129 = bf16[64,5,4096]{2,1,0:T(8,128)(2,1)} reshape(bf16[64,20480]{1,0:T(8,128)(2,1)} %convolution_convert_fusion) | data formatting | bytes 5242880 | tf_op jit(solution)/shard_map/reshape | solution.py:84
  143.1 21.4 %slice_reduce_fusion.8 = (bf16[64,4096]{1,0:T(8,128)(2,1)S(1)}, bf16[64,4096]{1,0:T(8,128)(2,1)S(1)}, bf16[64,4096]{1,0:T(8,128)(2,1)}, bf16[64,4096]{1,0:T(8,128)(2,1)}, bf16[64,4096]{1,0:T(8,128)(2,1)}) fusion(bf16[64,5,4096]{2,1,0:T(8,128)(2,1)} %reshape.129), kind=kLoop, calls=%fused_computation.33 | loop fusion | bytes 5242880 | tf_op jit(solution)/shard_map/slice | solution.py:17
  164.4 2.8 reshape.164
  167.2 2.8 reshape.163
  170.0 3.2 reshape.162
  173.1 2.1 reshape.165
  175.2 2.1 reshape.161
  177.3 21.6 %slice_reduce_fusion.9 = (bf16[64,4096]{1,0:T(8,128)(2,1)}, bf16[64,4096]{1,0:T(8,128)(2,1)}, bf16[64,4096]{1,0:T(8,128)(2,1)}, bf16[64,4096]{1,0:T(8,128)(2,1)}, bf16[64,4096]{1,0:T(8,128)(2,1)}) fusion(bf16[64,5,4096]{2,1,0:T(8,128)(2,1)} %all-to-all-done), kind=kLoop, calls=%fused_computation.34 | loop fusion | bytes 5242880 | tf_op jit(solution)/shard_map/slice | solution.py:13
  198.9 2.1 reshape_squeeze.36
  200.9 0.0 all-to-all-done.1
  200.9 2.0 convolution_convert_fusion.2
  203.0 7.2 %reshape.132 = bf16[64,64,4,64]{3,2,1,0:T(4,128)(2,1)} reshape(bf16[64,64,256]{2,1,0:T(8,128)(2,1)} %convolution_convert_fusion.2) | data formatting | bytes 4194304 | tf_op jit(solution)/shard_map/reshape | solution.py:20
  210.2 2.1 reshape_squeeze.34
  212.2 2.0 convolution_convert_fusion.3
  214.3 7.1 %reshape.131 = bf16[64,64,4,64]{3,2,1,0:T(4,128)(2,1)} reshape(bf16[64,64,256]{2,1,0:T(8,128)(2,1)} %convolution_convert_fusion.3) | data formatting | bytes 4194304 | tf_op jit(solution)/shard_map/reshape | solution.py:20
  221.4 2.1 reshape_squeeze.32
  223.4 2.0 convolution_convert_fusion.4
  225.5 7.1 %reshape.130 = bf16[64,64,4,64]{3,2,1,0:T(4,128)(2,1)} reshape(bf16[64,64,256]{2,1,0:T(8,128)(2,1)} %convolution_convert_fusion.4) | data formatting | bytes 4194304 | tf_op jit(solution)/shard_map/reshape | solution.py:20
  232.5 2.1 reshape_squeeze.38
  234.6 2.0 convolution_convert_fusion.1
  236.6 7.1 %reshape.133 = bf16[64,64,4,64]{3,2,1,0:T(4,128)(2,1)} reshape(bf16[64,64,256]{2,1,0:T(8,128)(2,1)} %convolution_convert_fusion.1) | data formatting | bytes 4194304 | tf_op jit(solution)/shard_map/reshape | solution.py:20
  243.7 2.3 reshape_squeeze.30
  245.9 2.0 convolution_convert_fusion.5
  247.9 7.2 %reshape.127 = bf16[64,64,4,64]{3,2,1,0:T(4,128)(2,1)} reshape(bf16[64,64,256]{2,1,0:T(8,128)(2,1)} %convolution_convert_fusion.5) | data formatting | bytes 4194304 | tf_op jit(solution)/shard_map/reshape | solution.py:20
  255.1 6.8 %fusion.3 = f32[64,64,4,64]{3,1,2,0:T(8,128)} fusion(bf16[64,64,4,64]{3,2,1,0:T(4,128)(2,1)} %reshape.132, bf16[64,64,64,1]{2,1,0,3:T(8,128)(2,1)S(1)} %copy-done.9), kind=kOutput, calls=%fused_computation.9 | convolution fusion | flops 134217728 | bytes 6815744 | tf_op jit(solution)/shard_map/plvr,psr->plvs/dot_general | solution.py:18
  261.9 0.0 copy-done.2
  262.0 4.5 %fusion.5 = f32[64,64,4,64]{3,1,2,0:T(8,128)} fusion(bf16[64,64,4,64]{3,2,1,0:T(4,128)(2,1)S(1)} %copy-done.2, bf16[64,64,64,1]{2,1,0,3:T(8,128)(2,1)S(1)} %copy-done.8), kind=kOutput, calls=%fused_computation.11 | convolution fusion | flops 134217728 | bytes 6815744 | tf_op jit(solution)/shard_map/plvr,psr->plvs/dot_general | solution.py:18
  266.4 0.0 copy-done.7
  266.4 4.5 %fusion.7 = f32[64,64,4,64]{3,1,2,0:T(8,128)} fusion(bf16[64,64,4,64]{3,2,1,0:T(4,128)(2,1)S(1)} %copy-done.3, bf16[64,64,64,1]{2,1,0,3:T(8,128)(2,1)S(1)} %copy-done.7), kind=kOutput, calls=%fused_computation.13 | convolution fusion | flops 134217728 | bytes 6815744 | tf_op jit(solution)/shard_map/plvr,psr->plvs/dot_general | solution.py:18
  270.9 4.4 %fusion.1 = f32[64,64,4,64]{3,1,2,0:T(8,128)} fusion(bf16[64,64,4,64]{3,2,1,0:T(4,128)(2,1)S(1)} %copy-done.4, bf16[64,64,64,1]{2,1,0,3:T(8,128)(2,1)S(1)} %copy-done.6), kind=kOutput, calls=%fused_computation.7 | convolution fusion | flops 134217728 | bytes 6815744 | tf_op jit(solution)/shard_map/plvr,psr->plvs/dot_general | solution.py:18
  275.3 15.3 %add_convert_fusion = bf16[64,64,4,64]{3,1,2,0:T(8,128)(2,1)} fusion(f32[64,64,4,64]{3,1,2,0:T(8,128)} %fusion.1, f32[64,64,4,64]{3,1,2,0:T(8,128)} %fusion.3, f32[64,64,4,64]{3,1,2,0:T(8,128)} %fusion.5, f32[64,64,4,64]{3,1,2,0:T(8,128)} %fusion.7, bf16[64,64,4,64]{3,2,1,0:T(4,128)(2,1)} %reshape.127, bf16[64,64,64,1]{2,1,0,3:T(8,128)(2,1)S(1)} %copy-done.10), kind=kOutput, calls=%fused_computation.4 | convolution fusion | flops 139460608 | bytes 21495808 | tf_op jit(solution)/shard_map/plvr,psr->plvs/dot_general | solution.py:18
  290.6 12.4 %copy.60 = bf16[64,64,4,64]{3,2,1,0:T(4,128)(2,1)} copy(bf16[64,64,4,64]{3,1,2,0:T(8,128)(2,1)} %add_convert_fusion) | data formatting | bytes 4194304 | tf_op jit(solution)/shard_map/convert_element_type | solution.py:24
  303.1 7.0 %convert_element_type.58 = bf16[64,64,256]{2,1,0:T(8,128)(2,1)} reshape(bf16[64,64,4,64]{3,2,1,0:T(4,128)(2,1)} %copy.60) | data formatting | bytes 4194304 | tf_op jit(solution)/shard_map/convert_element_type | solution.py:24
  310.1 10.3 %all-to-all-start.2 = ((bf16[64,64,256]{2,1,0:T(8,128)(2,1)}), bf16[64,64,256]{2,1,0:T(8,128)(2,1)S(1)}, u32[]{:S(2)}, u32[]{:S(2)}) async-start(bf16[64,64,256]{2,1,0:T(8,128)(2,1)} %convert_element_type.58), calls=%async_computation.2 | async-start | bytes 4194304 | tf_op jit(solution)/shard_map/all_to_all | solution.py:92
  320.4 0.0 all-reduce.2.cloned.1.call-start
  320.5 51.2 %all-to-all-done.2 = bf16[64,64,256]{2,1,0:T(8,128)(2,1)S(1)} async-done(((bf16[64,64,256]{2,1,0:T(8,128)(2,1)}), bf16[64,64,256]{2,1,0:T(8,128)(2,1)S(1)}, u32[]{:S(2)}, u32[]{:S(2)}) %all-to-all-start.2) | async-done | bytes 2097184 | tf_op jit(solution)/shard_map/all_to_all | solution.py:92
  371.6 1.6 gather_fusion
  373.2 0.0 all-reduce.2.cloned.1.call-update
  373.2 47.6 %all-reduce.2.cloned.1.call-done = bf16[4,8,64,256]{3,2,1,0:T(8,128)(2,1)} async-done(((bf16[4,8,64,256]{3,2,1,0:T(8,128)(2,1)}), bf16[4,8,64,256]{3,2,1,0:T(8,128)(2,1)}) %all-reduce.2.cloned.1.call-update) | async-done | bytes 1048592 | tf_op jit(solution)/shard_map/psum | solution.py:94
  420.8 2.3 copy.83
  (23 shorter events, 0.1 us)
Async XLA Ops:
  6.5 127.6 %copy-start = (bf16[4,5,4096]{2,0,1:T(4,128)(2,1)S(1)}, bf16[4,5,4096]{2,0,1:T(4,128)(2,1)}, u32[]{:S(2)}) copy-start(bf16[4,5,4096]{2,0,1:T(4,128)(2,1)} %param.8) | copy-start | bytes 491524
  19.1 12.7 %copy-start.11 = (bf16[4,8,64,256]{3,2,1,0:T(8,128)(2,1)S(1)}, bf16[4,8,64,256]{3,2,1,0:T(8,128)(2,1)}, u32[]{:S(2)}) copy-start(bf16[4,8,64,256]{3,2,1,0:T(8,128)(2,1)} %param.6) | copy-start | bytes 3145732
  19.1 108.5 %all-to-all-start = ((bf16[64,5,4096]{2,1,0:T(8,128)(2,1)}), bf16[64,5,4096]{2,1,0:T(8,128)(2,1)}, u32[]{:S(2)}, u32[]{:S(2)}) async-start(bf16[64,5,4096]{2,1,0:T(8,128)(2,1)} %scatter_fusion), calls=%async_computation | async-start | bytes 8388608 | tf_op jit(solution)/shard_map/all_to_all | solution.py:89
  33.4 1.4 copy-start.5
  127.6 73.3 %all-to-all-start.1 = ((bf16[64,64,256]{2,1,0:T(8,128)(2,1)}), bf16[64,64,256]{2,1,0:T(8,128)(2,1)S(1)}, u32[]{:S(2)}, u32[]{:S(2)}) async-start(bf16[64,64,256]{2,1,0:T(8,128)(2,1)} %copy-done.5), calls=%async_computation.1 | async-start | bytes 4194304 | tf_op jit(solution)/shard_map/all_to_all | solution.py:88
  247.9 7.2 %copy-start.9 = (bf16[64,64,64,1]{2,1,0,3:T(8,128)(2,1)S(1)}, bf16[64,64,64,1]{2,1,0,3:T(8,128)(2,1)}, u32[]{:S(2)}) copy-start(bf16[64,64,64,1]{2,1,0,3:T(8,128)(2,1)} %reshape.164) | copy-start | bytes 1572868
  255.1 6.8 %copy-start.2 = (bf16[64,64,4,64]{3,2,1,0:T(4,128)(2,1)S(1)}, bf16[64,64,4,64]{3,2,1,0:T(4,128)(2,1)}, u32[]{:S(2)}) copy-start(bf16[64,64,4,64]{3,2,1,0:T(4,128)(2,1)} %reshape.131) | copy-start | bytes 6291460
  255.1 6.8 %copy-start.8 = (bf16[64,64,64,1]{2,1,0,3:T(8,128)(2,1)S(1)}, bf16[64,64,64,1]{2,1,0,3:T(8,128)(2,1)}, u32[]{:S(2)}) copy-start(bf16[64,64,64,1]{2,1,0,3:T(8,128)(2,1)} %reshape.163) | copy-start | bytes 1572868
  261.9 4.5 %copy-start.3 = (bf16[64,64,4,64]{3,2,1,0:T(4,128)(2,1)S(1)}, bf16[64,64,4,64]{3,2,1,0:T(4,128)(2,1)}, u32[]{:S(2)}) copy-start(bf16[64,64,4,64]{3,2,1,0:T(4,128)(2,1)} %reshape.130) | copy-start | bytes 6291460
  261.9 4.5 %copy-start.7 = (bf16[64,64,64,1]{2,1,0,3:T(8,128)(2,1)S(1)}, bf16[64,64,64,1]{2,1,0,3:T(8,128)(2,1)}, u32[]{:S(2)}) copy-start(bf16[64,64,64,1]{2,1,0,3:T(8,128)(2,1)} %reshape.162) | copy-start | bytes 1572868
  266.4 4.5 %copy-start.4 = (bf16[64,64,4,64]{3,2,1,0:T(4,128)(2,1)S(1)}, bf16[64,64,4,64]{3,2,1,0:T(4,128)(2,1)}, u32[]{:S(2)}) copy-start(bf16[64,64,4,64]{3,2,1,0:T(4,128)(2,1)} %reshape.133) | copy-start | bytes 6291460
  266.4 4.5 %copy-start.6 = (bf16[64,64,64,1]{2,1,0,3:T(8,128)(2,1)S(1)}, bf16[64,64,64,1]{2,1,0,3:T(8,128)(2,1)}, u32[]{:S(2)}) copy-start(bf16[64,64,64,1]{2,1,0,3:T(8,128)(2,1)} %reshape.165) | copy-start | bytes 1572868
  270.9 4.5 %copy-start.10 = (bf16[64,64,64,1]{2,1,0,3:T(8,128)(2,1)S(1)}, bf16[64,64,64,1]{2,1,0,3:T(8,128)(2,1)}, u32[]{:S(2)}) copy-start(bf16[64,64,64,1]{2,1,0,3:T(8,128)(2,1)} %reshape.161) | copy-start | bytes 1572868
  303.1 120.0 %copy-start.1 = (bf16[4,5,4096]{2,0,1:T(4,128)(2,1)S(1)}, bf16[4,5,4096]{2,0,1:T(4,128)(2,1)}, u32[]{:S(2)}) copy-start(bf16[4,5,4096]{2,0,1:T(4,128)(2,1)} %param.8) | copy-start | bytes 491524
  310.1 61.6 %all-to-all-start.2 = ((bf16[64,64,256]{2,1,0:T(8,128)(2,1)}), bf16[64,64,256]{2,1,0:T(8,128)(2,1)S(1)}, u32[]{:S(2)}, u32[]{:S(2)}) async-start(bf16[64,64,256]{2,1,0:T(8,128)(2,1)} %convert_element_type.58), calls=%async_computation.2 | async-start | bytes 4194304 | tf_op jit(solution)/shard_map/all_to_all | solution.py:92
  320.4 100.4 %all-reduce.2.cloned.1.call-start = ((), (), s32[]{:S(2)}) async-start(), calls=%async_computation.3 | async-start | bytes 2097152 | tf_op jit(solution)/shard_map/psum | solution.py:94
Sparse Core Ops, SparseCore 0:
  373.4 47.3 all-reduce.1
where the time goes:
time: 436 us; the launch traced here: 430 us
  waiting for transfers between devices  192 us (44%)
  local copies, waits for them, and re-layouts  145 us (33%)
  matrix products  48.4 us (11%)
  starting transfers between devices  28.6 us (7%)
  between operations  14.1 us (3%)
    all_to_all x1, waiting for transfers between devices, per_device(): lax.all_to_all(send_left, 'bond', split_axis=0, concat_axis=0, tiled=True)  92.9 us
    all_to_all x1, waiting for transfers between devices, per_device(): lax.all_to_all(partial_sum, 'bond', split_axis=0, concat_axis=0, tiled=True)  51.2 us
    psum x1, waiting for transfers between devices, per_device(): summed = lax.psum(returned.astype(jnp.float32).astype(jnp.bfloat16), 'mpo')  47.6 us
    reshape x5, local copies, waits for them, and re-layouts, apply_terms(): sectioned.reshape(slot_count, block_width, vectors, block_width)  35.6 us
    dot_general x5, matrix products, apply_terms(): jnp.einsum('plvr,psr->plvs', sectioned.reshape(slot_count, block_width, v...  35.5 us
    slice x1, local copies, waits for them, and re-layouts, apply_terms(): left_term = left_rows[:, term].reshape(slot_count, block_width, block_width)  21.6 us
    slice x1, local copies, waits for them, and re-layouts, apply_terms(): right_rows[:, term].reshape(slot_count, block_width, block_width)  21.4 us
    convert_element_type x2, local copies, waits for them, and re-layouts, apply_terms(): summed.reshape(slot_count, block_width, column_count).astype(jnp.bfloat16)  19.4 us
  transfers between devices with their start and end apart: 4, of which 3 were waited for; matrix products, arithmetic and copies ran while one was open for 16% of the time, Pallas kernels for 0%

commit v1 on v0

v1 whole, which is shorter than its diff:
```python
import jax
import jax.numpy as jnp
from jax import lax
from jax.experimental import pallas as pl
from jax.experimental.pallas import tpu as pltpu
from jax.sharding import PartitionSpec as P


def block_kernel(gain_ref, wave_ref, left_ref, right_ref, out_ref):
    block_count, block_width, column_count = wave_ref.shape
    classes = gain_ref.shape[1]
    term_count = gain_ref.shape[0]
    rows = term_count * block_width
    vectors = column_count // block_width
    tile_rows = lax.broadcasted_iota(jnp.int32, (block_width, column_count), 0)
    tile_cols = lax.broadcasted_iota(jnp.int32, (block_width, column_count), 1)
    lane_tile = (tile_rows == tile_cols % block_width).astype(jnp.bfloat16)
    diag_rows = lax.broadcasted_iota(jnp.int32, (column_count, column_count), 0)
    diag_cols = lax.broadcasted_iota(jnp.int32, (column_count, column_count), 1)
    diagonal = diag_rows // block_width == diag_cols // block_width

    def body(b, carry):
        sector = b // classes
        charge = b % classes
        wave = wave_ref[b]
        scaled = []
        for w in range(term_count):
            piece = left_ref[sector, w * block_width:(w + 1) * block_width, :]
            scaled.append(
                (piece.astype(jnp.float32) * gain_ref[w, charge]).astype(jnp.bfloat16)
            )
        left_scaled = jnp.concatenate(scaled, axis=0)
        sectioned = jnp.dot(
            left_scaled, wave, preferred_element_type=jnp.float32
        ).astype(jnp.bfloat16)
        tiled = jnp.dot(
            right_ref[b], lane_tile, preferred_element_type=jnp.float32
        ).astype(jnp.bfloat16)
        acc = jnp.zeros((block_width, column_count), jnp.float32)
        for w in range(term_count):
            part = tiled[w * block_width:(w + 1) * block_width]
            expanded = jnp.concatenate([part] * vectors, axis=0)
            expanded = jnp.where(diagonal, expanded, jnp.zeros_like(expanded))
            acc = acc + jnp.dot(
                sectioned[w * block_width:(w + 1) * block_width],
                expanded,
                preferred_element_type=jnp.float32,
            )
        out_ref[b] = acc.astype(out_ref.dtype)
        return carry

    lax.fori_loop(0, block_count, body, 0)


def apply_blocks(gains, wave_rows, left_rows, right_rows):
    block_count, block_width, column_count = wave_rows.shape
    rows = right_rows.shape[1]
    flops = block_count * (
        2 * 2 * rows * block_width * column_count
        + 2 * rows * column_count * column_count
    )
    bytes_accessed = 2 * (
        2 * wave_rows.size + left_rows.size + right_rows.size
    )
    vmem = pltpu.MemorySpace.VMEM if hasattr(pltpu, "MemorySpace") else pltpu.VMEM
    return pl.pallas_call(
        block_kernel,
        out_shape=jax.ShapeDtypeStruct(wave_rows.shape, jnp.bfloat16),
        in_specs=[
            pl.BlockSpec(memory_space=pltpu.SMEM),
            pl.BlockSpec(memory_space=vmem),
            pl.BlockSpec(memory_space=vmem),
            pl.BlockSpec(memory_space=vmem),
        ],
        out_specs=pl.BlockSpec(memory_space=vmem),
        cost_estimate=pl.CostEstimate(
            flops=flops, bytes_accessed=bytes_accessed, transcendentals=0
        ),
    )(gains, wave_rows, left_rows, right_rows)


def per_device(wave_blocks, left_env, right_env, mpo_coef, mpo_mask, right_sector):
    sec_local, class_count, block_width, column_count = wave_blocks.shape
    term_local = left_env.shape[1]
    blocks_local = sec_local * class_count
    bond_count = lax.axis_size("bond")
    bond_index = lax.axis_index("bond")
    gains = mpo_coef * mpo_mask.astype(jnp.float32)

    requests = right_sector.reshape(bond_count, blocks_local)
    hits = (requests // sec_local) == bond_index
    send_sector = jnp.sum(
        jnp.where(hits, requests % sec_local, 0), axis=1
    ).astype(jnp.int32)
    right_t = jnp.swapaxes(
        right_env.reshape(sec_local, term_local, block_width, block_width), 2, 3
    ).reshape(sec_local, term_local, block_width * block_width)
    send_right = jnp.take(right_t, send_sector, axis=0)
    got_right = lax.all_to_all(send_right, "bond", split_axis=0, concat_axis=0, tiled=True)

    mine = lax.dynamic_slice_in_dim(requests, bond_index, 1, axis=0).reshape(blocks_local)
    right_rows = jnp.take(got_right, mine // sec_local, axis=0).reshape(
        blocks_local, term_local * block_width, block_width
    )
    left_rows = left_env.reshape(sec_local, term_local * block_width, block_width)
    wave_rows = wave_blocks.reshape(blocks_local, block_width, column_count)
    partial_sum = apply_blocks(gains, wave_rows, left_rows, right_rows)
    summed = lax.psum(partial_sum, "mpo")
    return summed.reshape(wave_blocks.shape)


def solution(mesh):
    return jax.shard_map(
        per_device,
        mesh=mesh,
        in_specs=(
            P("bond", None, None, None),
            P("bond", "mpo", None),
            P("bond", "mpo", None),
            P("mpo", None),
            P("mpo", None),
            P(),
        ),
        out_specs=P("bond", None, None, None),
        check_vma=False,
    )
```

time: 436 us -> 213 us (0.49); the launches traced: 430 us -> 213 us
  local copies, waits for them, and re-layouts: 145 us -> 16.8 us
  waiting for transfers between devices: 192 us -> 142 us
  matrix products: 48.4 us -> 0 us
  Pallas kernels: 0 us -> 20.8 us
  starting transfers between devices: 28.6 us -> 12.5 us
  other arithmetic: 2.51 us -> 7.97 us
    all_to_all x3 -> x1, waiting for transfers between devices: 144 us -> 93.9 us  [per_device(): lax.all_to_all(send_right, 'bond', split_axis=0, concat_axis=0, tiled=True)]
    dot_general x12 -> x0, matrix products: 48.4 us -> none  [the longest x5 35.5 us: apply_terms(): jnp.einsum('plvr,psr->plvs', sectioned.reshape(slot_count, block_width, v...]
    slice x2 -> x0, local copies, waits for them, and re-layouts: 43 us -> none  [the longest x1 21.6 us: apply_terms(): left_term = left_rows[:, term].reshape(slot_count, block_width, block_width)]
    reshape x8 -> x6, local copies, waits for them, and re-layouts: 42.3 us -> 2.95 us  [the longest x2 1.41 us: per_device(): right_env.reshape(sec_local, term_local, block_width, block_width)]
    another operation x10 -> x0, local copies, waits for them, and re-layouts: 23.3 us -> none  [the longest x5 12.8 us: apply_terms(): right_rows[:, term].reshape(slot_count, block_width, block_width)]
    pallas_call x0 -> x1, Pallas kernels: none -> 20.8 us  [apply_blocks(): pl.pallas_call(block_kernel, out_shape=jax.ShapeDtypeStruct(wave_rows.sha...]
    convert_element_type x3 -> x0, local copies, waits for them, and re-layouts: 20.5 us -> none  [the longest x2 19.4 us: apply_terms(): summed.reshape(slot_count, block_width, column_count).astype(jnp.bfloat16)]
    all_to_all x3 -> x1, starting transfers between devices: 28.5 us -> 12.4 us  [per_device(): lax.all_to_all(send_right, 'bond', split_axis=0, concat_axis=0, tiled=True)]
  transfers between devices with their start and end apart: 4 -> 2, of which waited for: 3 -> 2; matrix products, arithmetic and copies ran while one was open for 16% -> 1% of each run, Pallas kernels for 0% -> 0%
where the time goes in v1:
time: 213 us
  waiting for transfers between devices  142 us (67%)
  Pallas kernels  20.8 us (10%)
  local copies, waits for them, and re-layouts  16.8 us (8%)
  between operations  13.5 us (6%)
  starting transfers between devices  12.5 us (6%)
  other arithmetic  7.97 us (4%)
    all_to_all x1, waiting for transfers between devices, per_device(): lax.all_to_all(send_right, 'bond', split_axis=0, concat_axis=0, tiled=True)  93.9 us
    psum x1, waiting for transfers between devices, per_device(): summed = lax.psum(partial_sum, 'mpo')  47.5 us
    pallas_call x1, Pallas kernels, apply_blocks(): pl.pallas_call(block_kernel, out_shape=jax.ShapeDtypeStruct(wave_rows.sha...  20.8 us
    all_to_all x1, starting transfers between devices, per_device(): lax.all_to_all(send_right, 'bond', split_axis=0, concat_axis=0, tiled=True)  12.4 us
    gather x2, local copies, waits for them, and re-layouts, per_device(): jnp.take(got_right, mine // sec_local, axis=0)  8.44 us
    select_n x2, other arithmetic, per_device(): send_right = jnp.take(right_t, send_sector, axis=0)  4.68 us
  transfers between devices with their start and end apart: 2, of which 2 were waited for; matrix products, arithmetic and copies ran while one was open for 1% of the time, Pallas kernels for 0%

profile of v1, /device:TPU:8, one launch (start us, length us, event | category | flops | bytes accessed | tf_op | source)
XLA Modules:
  0.0 213.1 jit_solution(4350454396412049384)
XLA Ops:
  6.5 0.7 fusion.2
  7.3 0.1 reduce_sum.15
  7.4 0.1 reduce_sum.20
  7.5 1.2 reshape.133
  8.7 0.2 copy.14
  8.9 0.3 reshape.134
  9.2 0.1 copy.15
  9.3 2.8 %gather_fusion = bf16[64,5,4096]{2,1,0:T(8,128)(2,1)} fusion(bf16[4,5,4096]{2,1,0:T(8,128)(2,1)S(1)} %copy.15, s32[1024]{0:T(1024)S(1)} %pad_clamp_fusion.1), kind=kCustom, calls=%fused_computation | custom fusion | bytes 5243136 | tf_op jit(solution)/shard_map/jit(_take)/gather | solution.py:98
  12.1 4.7 %broadcast_select_fusion = bf16[64,5,4096]{2,1,0:T(8,128)(2,1)} fusion(bf16[64,5,4096]{2,1,0:T(8,128)(2,1)} %gather_fusion, pred[64]{0:T(512)(128)(4,1)S(1)} %compare_and_fusion), kind=kLoop, calls=%fused_computation.2 | loop fusion | flops 1310720 | bytes 5242944 | tf_op jit(solution)/shard_map/jit(_take)/select_n | solution.py:98
  16.8 0.0 copy-start.1
  16.8 0.0 copy-start
  16.8 0.0 copy-start.2
  16.8 0.0 copy-start.3
  16.8 12.4 %all-to-all-start = ((bf16[64,5,4096]{2,1,0:T(8,128)(2,1)}), bf16[64,5,4096]{2,1,0:T(8,128)(2,1)}, u32[]{:S(2)}, u32[]{:S(2)}) async-start(bf16[64,5,4096]{2,1,0:T(8,128)(2,1)} %broadcast_select_fusion), calls=%async_computation | async-start | bytes 8388608 | tf_op jit(solution)/shard_map/all_to_all | solution.py:99
  29.2 0.0 all-reduce.2.cloned.1.call-start
  29.3 0.0 copy-done.1
  29.3 0.1 copy.13
  29.4 0.1 reshape.131
  29.5 0.0 copy-done
  29.5 0.1 copy.12
  29.6 1.1 reshape.130.left_ref
  30.8 0.0 copy-done.2
  30.8 0.0 copy-done.3
  30.8 0.6 convert_multiply_fusion.gain_ref
  31.4 93.9 %all-to-all-done = bf16[64,5,4096]{2,1,0:T(8,128)(2,1)} async-done(((bf16[64,5,4096]{2,1,0:T(8,128)(2,1)}), bf16[64,5,4096]{2,1,0:T(8,128)(2,1)}, u32[]{:S(2)}, u32[]{:S(2)}) %all-to-all-start) | async-done | bytes 2621472 | tf_op jit(solution)/shard_map/all_to_all | solution.py:99
  125.3 4.2 %gather_fusion.1 = bf16[32,5,4096]{2,1,0:T(8,128)(2,1)} fusion(bf16[64,5,4096]{2,1,0:T(8,128)(2,1)} %all-to-all-done, s32[1024]{0:T(1024)S(1)} %pad_clamp_fusion), kind=kCustom, calls=%fused_computation.1 | custom fusion | bytes 2621568 | tf_op jit(solution)/shard_map/jit(_take)/gather | solution.py:102
  129.5 4.2 %gather.12 = bf16[32,320,64]{2,1,0:T(8,128)(2,1)S(1)} reshape(bf16[32,5,4096]{2,1,0:T(8,128)(2,1)} %gather_fusion.1) | data formatting | bytes 2621440 | tf_op jit(solution)/shard_map/jit(_take)/gather | solution.py:102
  133.8 1.8 broadcast_select_fusion.1.right_ref
  135.6 20.8 %shard_map.64 = bf16[32,64,256]{2,1,0:T(8,128)(2,1)} custom-call(f32[5,8]{1,0:T(8,128)} %convert_multiply_fusion.gain_ref, bf16[32,64,256]{2,1,0:T(8,128)(2,1)} %bitcast.37, bf16[4,320,64]{2,1,0:T(8,128)(2,1)} %reshape.130.left_ref, bf16[32,320,64]{2,1,0:T(8,128)(2,1)} %broadcast_select_fusion.1.right_ref), custom_call_target="tpu_custom_call" | custom-call | flops 2013265920 | bytes 3571712 | tf_op jit(solution)/shard_map/pallas_call | solution.py:66
  156.4 0.0 all-reduce.2.cloned.1.call-update
  156.4 47.5 %all-reduce.2.cloned.1.call-done = bf16[4,8,64,256]{3,2,1,0:T(8,128)(2,1)} async-done(((bf16[4,8,64,256]{3,2,1,0:T(8,128)(2,1)}), bf16[4,8,64,256]{3,2,1,0:T(8,128)(2,1)}) %all-reduce.2.cloned.1.call-update) | async-done | bytes 1048592 | tf_op jit(solution)/shard_map/psum | solution.py:108
  203.9 2.3 %copy.17 = bf16[4,8,64,256]{3,2,1,0:T(8,128)(2,1)} copy(bf16[4,8,64,256]{3,2,1,0:T(8,128)(2,1)} %all-reduce.2.cloned.1.call-done) | data formatting | bytes 2097152
  (6 shorter events, 0.1 us)
Async XLA Ops:
  16.8 12.5 %copy-start.1 = (s32[256,8]{0,1:T(8,128)S(1)}, s32[256,8]{0,1:T(8,128)}, u32[]{:S(2)}) copy-start(s32[256,8]{0,1:T(8,128)} %param.11) | copy-start | bytes 24580
  16.8 12.7 %copy-start = (bf16[4,5,4096]{2,0,1:T(4,128)(2,1)S(1)}, bf16[4,5,4096]{2,0,1:T(4,128)(2,1)}, u32[]{:S(2)}) copy-start(bf16[4,5,4096]{2,0,1:T(4,128)(2,1)} %param.7) | copy-start | bytes 491524
  16.8 14.0 %copy-start.2 = (f32[5,8]{1,0:T(8,128)S(1)}, f32[5,8]{1,0:T(8,128)}, u32[]{:S(2)}) copy-start(f32[5,8]{1,0:T(8,128)} %param.9) | copy-start | bytes 484
  16.8 14.0 %copy-start.3 = (s32[5,8]{1,0:T(8,128)S(1)}, s32[5,8]{1,0:T(8,128)}, u32[]{:S(2)}) copy-start(s32[5,8]{1,0:T(8,128)} %param.10) | copy-start | bytes 484
  16.8 108.5 %all-to-all-start = ((bf16[64,5,4096]{2,1,0:T(8,128)(2,1)}), bf16[64,5,4096]{2,1,0:T(8,128)(2,1)}, u32[]{:S(2)}, u32[]{:S(2)}) async-start(bf16[64,5,4096]{2,1,0:T(8,128)(2,1)} %broadcast_select_fusion), calls=%async_computation | async-start | bytes 8388608 | tf_op jit(solution)/shard_map/all_to_all | solution.py:99
  29.2 174.7 %all-reduce.2.cloned.1.call-start = ((), (), s32[]{:S(2)}) async-start(), calls=%async_computation.1 | async-start | bytes 2097152 | tf_op jit(solution)/shard_map/psum | solution.py:108
Sparse Core Ops, SparseCore 0:
  156.5 47.3 all-reduce.1

commit v2 on v1

--- a/solution.py
+++ b/solution.py
@@ -6,15 +6,20 @@
 from jax.sharding import PartitionSpec as P
 
 
-def block_kernel(gain_ref, wave_ref, left_ref, right_ref, out_ref):
+def block_kernel(gain_ref, source_ref, wave_ref, left_ref, right_ref, out_ref):
     block_count, block_width, column_count = wave_ref.shape
     classes = gain_ref.shape[1]
     term_count = gain_ref.shape[0]
     rows = term_count * block_width
     vectors = column_count // block_width
-    tile_rows = lax.broadcasted_iota(jnp.int32, (block_width, column_count), 0)
-    tile_cols = lax.broadcasted_iota(jnp.int32, (block_width, column_count), 1)
-    lane_tile = (tile_rows == tile_cols % block_width).astype(jnp.bfloat16)
+    lanes = right_ref.shape[2]
+    half_rows = block_width // 2
+    tile_rows = lax.broadcasted_iota(jnp.int32, (lanes, 2 * column_count), 0)
+    tile_cols = lax.broadcasted_iota(jnp.int32, (lanes, 2 * column_count), 1)
+    lane_tile = (
+        (tile_rows // block_width == tile_cols // column_count)
+        & (tile_rows % block_width == tile_cols % block_width)
+    ).astype(jnp.bfloat16)
     diag_rows = lax.broadcasted_iota(jnp.int32, (column_count, column_count), 0)
     diag_cols = lax.broadcasted_iota(jnp.int32, (column_count, column_count), 1)
     diagonal = diag_rows // block_width == diag_cols // block_width
@@ -34,11 +39,14 @@
             left_scaled, wave, preferred_element_type=jnp.float32
         ).astype(jnp.bfloat16)
         tiled = jnp.dot(
-            right_ref[b], lane_tile, preferred_element_type=jnp.float32
+            right_ref[source_ref[b]], lane_tile, preferred_element_type=jnp.float32
         ).astype(jnp.bfloat16)
         acc = jnp.zeros((block_width, column_count), jnp.float32)
         for w in range(term_count):
-            part = tiled[w * block_width:(w + 1) * block_width]
+            rows_w = tiled[w * half_rows:(w + 1) * half_rows]
+            part = jnp.concatenate(
+                [rows_w[:, :column_count], rows_w[:, column_count:]], axis=0
+            )
             expanded = jnp.concatenate([part] * vectors, axis=0)
             expanded = jnp.where(diagonal, expanded, jnp.zeros_like(expanded))
             acc = acc + jnp.dot(
@@ -52,9 +60,9 @@
     lax.fori_loop(0, block_count, body, 0)
 
 
-def apply_blocks(gains, wave_rows, left_rows, right_rows):
+def apply_blocks(gains, sources, wave_rows, left_rows, right_rows):
     block_count, block_width, column_count = wave_rows.shape
-    rows = right_rows.shape[1]
+    rows = left_rows.shape[1]
     flops = block_count * (
         2 * 2 * rows * block_width * column_count
         + 2 * rows * column_count * column_count
@@ -68,6 +76,7 @@
         out_shape=jax.ShapeDtypeStruct(wave_rows.shape, jnp.bfloat16),
         in_specs=[
             pl.BlockSpec(memory_space=pltpu.SMEM),
+            pl.BlockSpec(memory_space=pltpu.SMEM),
             pl.BlockSpec(memory_space=vmem),
             pl.BlockSpec(memory_space=vmem),
             pl.BlockSpec(memory_space=vmem),
@@ -76,7 +85,7 @@
         cost_estimate=pl.CostEstimate(
             flops=flops, bytes_accessed=bytes_accessed, transcendentals=0
         ),
-    )(gains, wave_rows, left_rows, right_rows)
+    )(gains, sources, wave_rows, left_rows, right_rows)
 
 
 def per_device(wave_blocks, left_env, right_env, mpo_coef, mpo_mask, right_sector):
@@ -92,19 +101,19 @@
     send_sector = jnp.sum(
         jnp.where(hits, requests % sec_local, 0), axis=1
     ).astype(jnp.int32)
-    right_t = jnp.swapaxes(
-        right_env.reshape(sec_local, term_local, block_width, block_width), 2, 3
-    ).reshape(sec_local, term_local, block_width * block_width)
-    send_right = jnp.take(right_t, send_sector, axis=0)
+    half_rows = block_width // 2
+    right_t = jnp.transpose(
+        right_env.reshape(sec_local, term_local, block_width, 2, half_rows),
+        (0, 1, 4, 3, 2),
+    ).reshape(sec_local, term_local * half_rows, 2 * block_width)
+    send_right = jnp.take(right_t, send_sector, axis=0, mode="clip")
     got_right = lax.all_to_all(send_right, "bond", split_axis=0, concat_axis=0, tiled=True)
 
     mine = lax.dynamic_slice_in_dim(requests, bond_index, 1, axis=0).reshape(blocks_local)
-    right_rows = jnp.take(got_right, mine // sec_local, axis=0).reshape(
-        blocks_local, term_local * block_width, block_width
-    )
+    sources = (mine // sec_local).astype(jnp.int32)
     left_rows = left_env.reshape(sec_local, term_local * block_width, block_width)
     wave_rows = wave_blocks.reshape(blocks_local, block_width, column_count)
-    partial_sum = apply_blocks(gains, wave_rows, left_rows, right_rows)
+    partial_sum = apply_blocks(gains, sources, wave_rows, left_rows, got_right)
     summed = lax.psum(partial_sum, "mpo")
     return summed.reshape(wave_blocks.shape)
 

time: 213 us -> 167 us (0.78)
  waiting for transfers between devices: 142 us -> 107 us
  local copies, waits for them, and re-layouts: 16.8 us -> 10.1 us
  other arithmetic: 7.97 us -> 1.96 us
    all_to_all x1, waiting for transfers between devices: 93.9 us -> 59.9 us  [per_device(): lax.all_to_all(send_right, 'bond', split_axis=0, concat_axis=0, tiled=True)]
    gather x3 -> x1, local copies, waits for them, and re-layouts: 11.2 us -> 2.4 us  [per_device(): send_right = jnp.take(right_t, send_sector, axis=0, mode='clip')]
    select_n x4 -> x1, other arithmetic: 6.51 us -> 0.53 us  [per_device(): sources = (mine // sec_local).astype(jnp.int32)]
where the time goes in v2:
time: 167 us
  waiting for transfers between devices  107 us (64%)
  Pallas kernels  21.5 us (13%)
  between operations  13.5 us (8%)
  starting transfers between devices  12.3 us (7%)
  local copies, waits for them, and re-layouts  10.1 us (6%)
  other arithmetic  1.96 us (1%)
    all_to_all x1, waiting for transfers between devices, per_device(): lax.all_to_all(send_right, 'bond', split_axis=0, concat_axis=0, tiled=True)  59.9 us
    psum x1, waiting for transfers between devices, per_device(): summed = lax.psum(partial_sum, 'mpo')  47.5 us
    pallas_call x1, Pallas kernels, apply_blocks(): pl.pallas_call(block_kernel, out_shape=jax.ShapeDtypeStruct(wave_rows.sha...  21.5 us
    all_to_all x1, starting transfers between devices, per_device(): lax.all_to_all(send_right, 'bond', split_axis=0, concat_axis=0, tiled=True)  12.2 us
    unnamed x13, local copies, waits for them, and re-layouts  4.05 us
  transfers between devices with their start and end apart: 2, of which 2 were waited for; matrix products, arithmetic and copies ran while one was open for 1% of the time, Pallas kernels for 0%

profile of v2, /device:TPU:8, one launch (start us, length us, event | category | flops | bytes accessed | tf_op | source)
XLA Modules:
  0.0 166.7 jit_solution(5524741471645629761)
XLA Ops:
  6.5 0.7 fusion.2
  7.3 0.1 reduce_sum.14
  7.4 0.1 reduce_sum.18
  7.5 1.3 reshape.26
  8.8 0.9 copy.10
  9.8 0.2 reshape.27
  9.9 2.4 %gather_fusion = bf16[64,160,128]{2,1,0:T(8,128)(2,1)} fusion(bf16[4,160,128]{2,1,0:T(8,128)(2,1)S(1)} %reshape.27, s32[1024]{0:T(1024)S(1)} %pad_clamp_fusion), kind=kCustom, calls=%fused_computation | custom fusion | bytes 5243136 | tf_op jit(solution)/shard_map/jit(_take)/gather | solution.py:109
  12.3 0.0 copy-start.2
  12.3 0.0 copy-start.1
  12.3 0.0 copy-start.3
  12.4 0.0 copy-start.4
  12.4 12.2 %all-to-all-start = ((bf16[64,160,128]{2,1,0:T(8,128)(2,1)}), bf16[64,160,128]{2,1,0:T(8,128)(2,1)S(1)}, u32[]{:S(2)}, u32[]{:S(2)}) async-start(bf16[64,160,128]{2,1,0:T(8,128)(2,1)} %gather_fusion), calls=%async_computation | async-start | bytes 5242880 | tf_op jit(solution)/shard_map/all_to_all | solution.py:110
  24.6 0.0 all-reduce.2.cloned.1.call-start
  24.7 0.0 copy-done.2
  24.7 0.1 copy.8
  24.8 0.1 reshape.22
  24.9 0.0 copy-done.1
  24.9 0.1 copy.9
  25.0 1.1 reshape.25.left_ref
  26.1 0.5 and_select_fusion.source_ref
  26.6 0.0 copy-done.3
  26.6 0.0 copy-done.4
  26.6 0.6 convert_multiply_fusion.gain_ref
  27.2 59.9 %all-to-all-done.right_ref = bf16[64,160,128]{2,1,0:T(8,128)(2,1)S(1)} async-done(((bf16[64,160,128]{2,1,0:T(8,128)(2,1)}), bf16[64,160,128]{2,1,0:T(8,128)(2,1)S(1)}, u32[]{:S(2)}, u32[]{:S(2)}) %all-to-all-start) | async-done | bytes 2621472 | tf_op jit(solution)/shard_map/all_to_all | solution.py:110
  87.1 0.0 copy-start
  87.1 1.5 copy-done
  88.6 21.5 %shard_map.64 = bf16[32,64,256]{2,1,0:T(8,128)(2,1)} custom-call(f32[5,8]{1,0:T(8,128)} %convert_multiply_fusion.gain_ref, s32[32]{0:T(128)} %and_select_fusion.source_ref, bf16[32,64,256]{2,1,0:T(8,128)(2,1)} %bitcast.15, bf16[4,320,64]{2,1,0:T(8,128)(2,1)} %reshape.25.left_ref, bf16[64,160,128]{2,1,0:T(8,128)(2,1)} %copy-done), custom_call_target="tpu_custom_call" | custom-call | flops 2013265920 | bytes 4882432 | tf_op jit(solution)/shard_map/pallas_call | solution.py:74
  110.0 0.0 all-reduce.2.cloned.1.call-update
  110.1 47.5 %all-reduce.2.cloned.1.call-done = bf16[4,8,64,256]{3,2,1,0:T(8,128)(2,1)} async-done(((bf16[4,8,64,256]{3,2,1,0:T(8,128)(2,1)}), bf16[4,8,64,256]{3,2,1,0:T(8,128)(2,1)}) %all-reduce.2.cloned.1.call-update) | async-done | bytes 1048592 | tf_op jit(solution)/shard_map/psum | solution.py:117
  157.6 2.3 %copy.12 = bf16[4,8,64,256]{3,2,1,0:T(8,128)(2,1)} copy(bf16[4,8,64,256]{3,2,1,0:T(8,128)(2,1)} %all-reduce.2.cloned.1.call-done) | data formatting | bytes 2097152
  (1 shorter events, 0.0 us)
Async XLA Ops:
  12.3 12.3 %copy-start.2 = (s32[256,8]{0,1:T(8,128)S(1)}, s32[256,8]{0,1:T(8,128)}, u32[]{:S(2)}) copy-start(s32[256,8]{0,1:T(8,128)} %param.11) | copy-start | bytes 24580
  12.3 12.6 %copy-start.1 = (bf16[4,5,4096]{2,0,1:T(4,128)(2,1)S(1)}, bf16[4,5,4096]{2,0,1:T(4,128)(2,1)}, u32[]{:S(2)}) copy-start(bf16[4,5,4096]{2,0,1:T(4,128)(2,1)} %param.7) | copy-start | bytes 491524
  12.3 14.2 %copy-start.3 = (f32[5,8]{1,0:T(8,128)S(1)}, f32[5,8]{1,0:T(8,128)}, u32[]{:S(2)}) copy-start(f32[5,8]{1,0:T(8,128)} %param.9) | copy-start | bytes 484
  12.4 14.3 %copy-start.4 = (s32[5,8]{1,0:T(8,128)S(1)}, s32[5,8]{1,0:T(8,128)}, u32[]{:S(2)}) copy-start(s32[5,8]{1,0:T(8,128)} %param.10) | copy-start | bytes 484
  12.4 74.7 %all-to-all-start = ((bf16[64,160,128]{2,1,0:T(8,128)(2,1)}), bf16[64,160,128]{2,1,0:T(8,128)(2,1)S(1)}, u32[]{:S(2)}, u32[]{:S(2)}) async-start(bf16[64,160,128]{2,1,0:T(8,128)(2,1)} %gather_fusion), calls=%async_computation | async-start | bytes 5242880 | tf_op jit(solution)/shard_map/all_to_all | solution.py:110
  24.6 132.9 %all-reduce.2.cloned.1.call-start = ((), (), s32[]{:S(2)}) async-start(), calls=%async_computation.1 | async-start | bytes 2097152 | tf_op jit(solution)/shard_map/psum | solution.py:117
  87.1 1.5 copy-start
Sparse Core Ops, SparseCore 0:
  110.2 47.3 all-reduce.1

commit v3 on v2

--- a/solution.py
+++ b/solution.py
@@ -114,8 +114,20 @@
     left_rows = left_env.reshape(sec_local, term_local * block_width, block_width)
     wave_rows = wave_blocks.reshape(blocks_local, block_width, column_count)
     partial_sum = apply_blocks(gains, sources, wave_rows, left_rows, got_right)
-    summed = lax.psum(partial_sum, "mpo")
-    return summed.reshape(wave_blocks.shape)
+    mpo_count = lax.axis_size("mpo")
+    mpo_index = lax.axis_index("mpo")
+    parts = [partial_sum]
+    for shift in range(1, mpo_count):
+        pairs = [(i, (i + shift) % mpo_count) for i in range(mpo_count)]
+        parts.append(lax.ppermute(partial_sum, "mpo", pairs))
+    stacked = jnp.stack(parts)
+    summed = jnp.zeros(partial_sum.shape, jnp.float32)
+    for group in range(mpo_count):
+        at = (mpo_index - group) % mpo_count
+        summed = summed + lax.dynamic_index_in_dim(
+            stacked, at, 0, keepdims=False
+        ).astype(jnp.float32)
+    return summed.astype(jnp.bfloat16).reshape(wave_blocks.shape)
 
 
 def solution(mesh):

time: 167 us -> 158 us (0.946)
  between operations: 13.5 us -> 0.11 us
  starting transfers between devices: 12.3 us -> 16.7 us
  other arithmetic: 1.96 us -> 5.27 us
  local copies, waits for them, and re-layouts: 10.1 us -> 7.8 us
  waiting for transfers between devices: 107 us -> 105 us
    psum x1 -> x0, waiting for transfers between devices: 47.5 us -> none  [per_device(): summed = lax.psum(partial_sum, 'mpo')]
    ppermute x0 -> x3, waiting for transfers between devices: none -> 45.5 us  [per_device(): parts.append(lax.ppermute(partial_sum, 'mpo', pairs))]
    ppermute x0 -> x3, starting transfers between devices: none -> 4.45 us  [per_device(): parts.append(lax.ppermute(partial_sum, 'mpo', pairs))]
    another operation x0 -> x2, other arithmetic: none -> 3.32 us
    unnamed x13 -> x12, local copies, waits for them, and re-layouts: 4.05 us -> 1.73 us
  transfers between devices with their start and end apart: 2 -> 4, of which waited for: 2 -> 3; matrix products, arithmetic and copies ran while one was open for 1% -> 2% of each run, Pallas kernels for 0% -> 0%
where the time goes in v3:
time: 158 us; the launch traced here: 157 us
  waiting for transfers between devices  105 us (66%)
  Pallas kernels  21.5 us (14%)
  starting transfers between devices  16.7 us (11%)
  local copies, waits for them, and re-layouts  7.8 us (5%)
  other arithmetic  5.27 us (3%)
    all_to_all x1, waiting for transfers between devices, per_device(): lax.all_to_all(send_right, 'bond', split_axis=0, concat_axis=0, tiled=True)  60 us
    ppermute x3, waiting for transfers between devices, per_device(): parts.append(lax.ppermute(partial_sum, 'mpo', pairs))  45.5 us
    pallas_call x1, Pallas kernels, apply_blocks(): pl.pallas_call(block_kernel, out_shape=jax.ShapeDtypeStruct(wave_rows.sha...  21.5 us
    all_to_all x1, starting transfers between devices, per_device(): lax.all_to_all(send_right, 'bond', split_axis=0, concat_axis=0, tiled=True)  12.2 us
    ppermute x3, starting transfers between devices, per_device(): parts.append(lax.ppermute(partial_sum, 'mpo', pairs))  4.45 us
  transfers between devices with their start and end apart: 4, of which 3 were waited for; matrix products, arithmetic and copies ran while one was open for 2% of the time, Pallas kernels for 0%

profile of v3, /device:TPU:8, one launch (start us, length us, event | category | flops | bytes accessed | tf_op | source)
XLA Modules:
  0.0 156.7 jit_solution(15605640755920764270)
XLA Ops:
  0.0 1.3 reshape.36
  1.3 0.9 copy.10
  2.3 0.2 reshape.37
  2.5 0.7 fusion.2
  3.2 0.1 reduce_sum.14
  3.3 0.1 reduce_sum.18
  3.4 2.4 %gather_fusion = bf16[64,160,128]{2,1,0:T(8,128)(2,1)} fusion(bf16[4,160,128]{2,1,0:T(8,128)(2,1)S(1)} %reshape.37, s32[1024]{0:T(1024)S(1)} %pad_clamp_fusion), kind=kCustom, calls=%fused_computation | custom fusion | bytes 5243136 | tf_op jit(solution)/shard_map/jit(_take)/gather | solution.py:109
  5.8 0.0 copy-start.2
  5.8 0.0 copy-start.1
  5.8 0.0 copy-start.3
  5.8 0.0 copy-start.4
  5.8 12.2 %all-to-all-start = ((bf16[64,160,128]{2,1,0:T(8,128)(2,1)}), bf16[64,160,128]{2,1,0:T(8,128)(2,1)S(1)}, u32[]{:S(2)}, u32[]{:S(2)}) async-start(bf16[64,160,128]{2,1,0:T(8,128)(2,1)} %gather_fusion), calls=%async_computation | async-start | bytes 5242880 | tf_op jit(solution)/shard_map/all_to_all | solution.py:110
  18.1 0.0 copy-done.2
  18.1 0.1 copy.8
  18.2 0.1 reshape.32
  18.3 0.0 copy-done.1
  18.3 0.1 copy.9
  18.4 1.0 reshape.35.left_ref
  19.5 0.5 and_select_fusion.source_ref
  20.0 0.0 copy-done.3
  20.0 0.0 copy-done.4
  20.0 0.6 convert_multiply_fusion.gain_ref
  20.6 60.0 %all-to-all-done.right_ref = bf16[64,160,128]{2,1,0:T(8,128)(2,1)S(1)} async-done(((bf16[64,160,128]{2,1,0:T(8,128)(2,1)}), bf16[64,160,128]{2,1,0:T(8,128)(2,1)S(1)}, u32[]{:S(2)}, u32[]{:S(2)}) %all-to-all-start) | async-done | bytes 2621472 | tf_op jit(solution)/shard_map/all_to_all | solution.py:110
  80.5 0.0 copy-start
  80.5 1.5 copy-done
  82.0 21.5 %shard_map.64 = bf16[32,64,256]{2,1,0:T(8,128)(2,1)} custom-call(f32[5,8]{1,0:T(8,128)} %convert_multiply_fusion.gain_ref, s32[32]{0:T(128)} %and_select_fusion.source_ref, bf16[32,64,256]{2,1,0:T(8,128)(2,1)} %bitcast.18, bf16[4,320,64]{2,1,0:T(8,128)(2,1)} %reshape.35.left_ref, bf16[64,160,128]{2,1,0:T(8,128)(2,1)} %copy-done), custom_call_target="tpu_custom_call" | custom-call | flops 2013265920 | bytes 4882432 | tf_op jit(solution)/shard_map/pallas_call | solution.py:74
  103.5 2.8 %collective-permute-start.2 = (bf16[32,64,256]{2,1,0:T(8,128)(2,1)}, bf16[32,64,256]{2,1,0:T(8,128)(2,1)S(1)}, u32[]{:S(2)}, u32[]{:S(2)}) collective-permute-start(bf16[32,64,256]{2,1,0:T(8,128)(2,1)} %shard_map.64), channel_id=1, source_target_pairs={{0,3},{1,0},{2,1},{3,2},{4,7},{5,4},{6,5},{7,6},{8,11},{9,8},{10,9... | collective-permute-start | bytes 3145736 | tf_op jit(solution)/shard_map/ppermute | solution.py:122
  106.3 0.8 collective-permute-start.1
  107.1 0.9 collective-permute-start
  107.9 41.9 %collective-permute-done.2 = bf16[32,64,256]{2,1,0:T(8,128)(2,1)S(1)} collective-permute-done((bf16[32,64,256]{2,1,0:T(8,128)(2,1)}, bf16[32,64,256]{2,1,0:T(8,128)(2,1)S(1)}, u32[]{:S(2)}, u32[]{:S(2)}) %collective-permute-start.2) | collective-permute-done | bytes 1048608 | tf_op jit(solution)/shard_map/ppermute | solution.py:122
  149.8 0.0 collective-permute-done.1
  149.8 3.6 %collective-permute-done = bf16[32,64,256]{2,1,0:T(8,128)(2,1)S(1)} collective-permute-done((bf16[32,64,256]{2,1,0:T(8,128)(2,1)}, bf16[32,64,256]{2,1,0:T(8,128)(2,1)S(1)}, u32[]{:S(2)}, u32[]{:S(2)}) %collective-permute-start) | collective-permute-done | bytes 1048608 | tf_op jit(solution)/shard_map/ppermute | solution.py:122
  153.4 1.6 %pad_maximum_fusion = bf16[4,32,64,256]{3,2,1,0:T(8,128)(2,1)S(1)} fusion(bf16[1,32,64,256]{3,2,1,0:T(8,128)(2,1)S(1)} %bitcast.15, bf16[1,32,64,256]{3,2,1,0:T(8,128)(2,1)S(1)} %bitcast.16, bf16[1,32,64,256]{3,2,1,0:T(8,128)(2,1)S(1)} %bitcast.17, bf16[1,32,64,256]{3,2,1,0:T(8,128)(2,1)} %bitcast.14), kind=kLoop, calls=%fused_computation.1 | loop fusion | flops 6291456 | bytes 8388608 | tf_op jit(solution)/shard_map/stack | solution.py:123
  155.0 1.7 %add_convert_fusion = bf16[1,32,64,256]{3,2,1,0:T(8,128)(2,1)} fusion(bf16[4,32,64,256]{3,2,1,0:T(8,128)(2,1)S(1)} %pad_maximum_fusion, s32[]{:T(128)S(6)} %select_n.70, s32[]{:T(128)S(6)} %select_n.68, s32[]{:T(128)S(6)} %select_n.66, s32[]{:T(128)S(6)} %select_n.64), kind=kLoop, calls=%fused_computation.2 | loop fusion | flops 4194304 | bytes 5242896 | tf_op jit(solution)/shard_map/convert
  (1 shorter events, 0.0 us)
Async XLA Ops:
  5.8 12.3 %copy-start.2 = (s32[256,8]{0,1:T(8,128)S(1)}, s32[256,8]{0,1:T(8,128)}, u32[]{:S(2)}) copy-start(s32[256,8]{0,1:T(8,128)} %param.11) | copy-start | bytes 24580
  5.8 12.5 %copy-start.1 = (bf16[4,5,4096]{2,0,1:T(4,128)(2,1)S(1)}, bf16[4,5,4096]{2,0,1:T(4,128)(2,1)}, u32[]{:S(2)}) copy-start(bf16[4,5,4096]{2,0,1:T(4,128)(2,1)} %param.7) | copy-start | bytes 491524
  5.8 14.2 %copy-start.3 = (f32[5,8]{1,0:T(8,128)S(1)}, f32[5,8]{1,0:T(8,128)}, u32[]{:S(2)}) copy-start(f32[5,8]{1,0:T(8,128)} %param.9) | copy-start | bytes 484
  5.8 14.2 %copy-start.4 = (s32[5,8]{1,0:T(8,128)S(1)}, s32[5,8]{1,0:T(8,128)}, u32[]{:S(2)}) copy-start(s32[5,8]{1,0:T(8,128)} %param.10) | copy-start | bytes 484
  5.8 74.7 %all-to-all-start = ((bf16[64,160,128]{2,1,0:T(8,128)(2,1)}), bf16[64,160,128]{2,1,0:T(8,128)(2,1)S(1)}, u32[]{:S(2)}, u32[]{:S(2)}) async-start(bf16[64,160,128]{2,1,0:T(8,128)(2,1)} %gather_fusion), calls=%async_computation | async-start | bytes 5242880 | tf_op jit(solution)/shard_map/all_to_all | solution.py:110
  80.5 1.5 copy-start
  103.5 46.3 %collective-permute-start.2 = (bf16[32,64,256]{2,1,0:T(8,128)(2,1)}, bf16[32,64,256]{2,1,0:T(8,128)(2,1)S(1)}, u32[]{:S(2)}, u32[]{:S(2)}) collective-permute-start(bf16[32,64,256]{2,1,0:T(8,128)(2,1)} %shard_map.64), channel_id=1, source_target_pairs={{0,3},{1,0},{2,1},{3,2},{4,7},{5,4},{6,5},{7,6},{8,11},{9,8},{10,9... | collective-permute-start | bytes 3145736 | tf_op jit(solution)/shard_map/ppermute | solution.py:122
  106.3 43.6 %collective-permute-start.1 = (bf16[32,64,256]{2,1,0:T(8,128)(2,1)}, bf16[32,64,256]{2,1,0:T(8,128)(2,1)S(1)}, u32[]{:S(2)}, u32[]{:S(2)}) collective-permute-start(bf16[32,64,256]{2,1,0:T(8,128)(2,1)} %shard_map.64), channel_id=1, source_target_pairs={{0,2},{1,3},{2,0},{3,1},{4,6},{5,7},{6,4},{7,5},{8,10},{9,11},{10,... | collective-permute-start | bytes 3145736 | tf_op jit(solution)/shard_map/ppermute | solution.py:122
  107.1 46.4 %collective-permute-start = (bf16[32,64,256]{2,1,0:T(8,128)(2,1)}, bf16[32,64,256]{2,1,0:T(8,128)(2,1)S(1)}, u32[]{:S(2)}, u32[]{:S(2)}) collective-permute-start(bf16[32,64,256]{2,1,0:T(8,128)(2,1)} %shard_map.64), channel_id=1, source_target_pairs={{0,1},{1,2},{2,3},{3,0},{4,5},{5,6},{6,7},{7,4},{8,9},{9,10},{10,1... | collective-permute-start | bytes 3145736 | tf_op jit(solution)/shard_map/ppermute | solution.py:122

commit v4 on v2

v4 whole, which is shorter than its diff:
```python
import jax
import jax.numpy as jnp
from jax import lax
from jax.experimental import pallas as pl
from jax.experimental.pallas import tpu as pltpu
from jax.sharding import PartitionSpec as P


def block_kernel(gain_ref, wave_ref, left_ref, right_ref, out_ref):
    block_count, block_width, column_count = wave_ref.shape
    group_count = left_ref.shape[0]
    term_count = gain_ref.shape[0] // group_count
    vectors = column_count // block_width
    lanes = right_ref.shape[3]
    half_rows = block_width // 2
    tile_rows = lax.broadcasted_iota(jnp.int32, (lanes, 2 * column_count), 0)
    tile_cols = lax.broadcasted_iota(jnp.int32, (lanes, 2 * column_count), 1)
    lane_tile = (
        (tile_rows // block_width == tile_cols // column_count)
        & (tile_rows % block_width == tile_cols % block_width)
    ).astype(jnp.bfloat16)
    diag_rows = lax.broadcasted_iota(jnp.int32, (column_count, column_count), 0)
    diag_cols = lax.broadcasted_iota(jnp.int32, (column_count, column_count), 1)
    diagonal = diag_rows // block_width == diag_cols // block_width

    def body(b, carry):
        wave = wave_ref[b]
        total = jnp.zeros((block_width, column_count), jnp.float32)
        for g in range(group_count):
            scaled = []
            for w in range(term_count):
                piece = left_ref[g, w * block_width:(w + 1) * block_width, :]
                gain = gain_ref[g * term_count + w, b]
                scaled.append((piece.astype(jnp.float32) * gain).astype(jnp.bfloat16))
            left_scaled = jnp.concatenate(scaled, axis=0)
            sectioned = jnp.dot(
                left_scaled, wave, preferred_element_type=jnp.float32
            ).astype(jnp.bfloat16)
            tiled = jnp.dot(
                right_ref[g, b], lane_tile, preferred_element_type=jnp.float32
            ).astype(jnp.bfloat16)
            acc = jnp.zeros((block_width, column_count), jnp.float32)
            for w in range(term_count):
                rows_w = tiled[w * half_rows:(w + 1) * half_rows]
                part = jnp.concatenate(
                    [rows_w[:, :column_count], rows_w[:, column_count:]], axis=0
                )
                expanded = jnp.concatenate([part] * vectors, axis=0)
                expanded = jnp.where(diagonal, expanded, jnp.zeros_like(expanded))
                acc = acc + jnp.dot(
                    sectioned[w * block_width:(w + 1) * block_width],
                    expanded,
                    preferred_element_type=jnp.float32,
                )
            total = total + acc.astype(jnp.bfloat16).astype(jnp.float32)
        out_ref[b] = total.astype(out_ref.dtype)
        return carry

    lax.fori_loop(0, block_count, body, 0)


def apply_blocks(gains, wave_rows, left_rows, right_rows):
    block_count, block_width, column_count = wave_rows.shape
    group_count, rows = left_rows.shape[0], left_rows.shape[1]
    flops = block_count * group_count * (
        2 * 2 * rows * block_width * column_count
        + 2 * rows * column_count * column_count
    )
    bytes_accessed = 2 * (
        2 * wave_rows.size + left_rows.size + right_rows.size
    )
    vmem = pltpu.MemorySpace.VMEM if hasattr(pltpu, "MemorySpace") else pltpu.VMEM
    return pl.pallas_call(
        block_kernel,
        out_shape=jax.ShapeDtypeStruct(wave_rows.shape, jnp.bfloat16),
        in_specs=[
            pl.BlockSpec(memory_space=pltpu.SMEM),
            pl.BlockSpec(memory_space=vmem),
            pl.BlockSpec(memory_space=vmem),
            pl.BlockSpec(memory_space=vmem),
        ],
        out_specs=pl.BlockSpec(memory_space=vmem),
        cost_estimate=pl.CostEstimate(
            flops=flops, bytes_accessed=bytes_accessed, transcendentals=0
        ),
    )(gains, wave_rows, left_rows, right_rows)


def shifted(value, shift, count):
    pairs = [(i, (i + shift) % count) for i in range(count)]
    return lax.ppermute(value, "mpo", pairs)


def per_device(wave_blocks, left_env, right_env, mpo_coef, mpo_mask, right_sector):
    sec_local, class_count, block_width, column_count = wave_blocks.shape
    term_local = left_env.shape[1]
    blocks_local = sec_local * class_count
    bond_count = lax.axis_size("bond")
    bond_index = lax.axis_index("bond")
    mpo_count = lax.axis_size("mpo")
    mpo_index = lax.axis_index("mpo")
    half_rows = block_width // 2
    gains = mpo_coef * mpo_mask.astype(jnp.float32)

    requests = right_sector.reshape(bond_count, blocks_local)
    hits = (requests // sec_local) == bond_index
    send_sector = jnp.sum(
        jnp.where(hits, requests % sec_local, 0), axis=1
    ).astype(jnp.int32)
    right_t = jnp.transpose(
        right_env.reshape(sec_local, term_local, block_width, 2, half_rows),
        (0, 1, 4, 3, 2),
    ).reshape(sec_local, term_local * half_rows, 2 * block_width)
    send_right = jnp.take(right_t, send_sector, axis=0, mode="clip")
    got_right = lax.all_to_all(send_right, "bond", split_axis=0, concat_axis=0, tiled=True)

    left_flat = left_env.reshape(sec_local, term_local * half_rows, 2 * block_width)
    left_parts = [lax.dynamic_index_in_dim(left_flat, mpo_index, 0, keepdims=False)]
    gain_parts = [gains]
    for shift in range(1, mpo_count):
        target = (mpo_index + shift) % mpo_count
        left_parts.append(
            shifted(lax.dynamic_index_in_dim(left_flat, target, 0, keepdims=False), shift, mpo_count)
        )
        gain_parts.append(shifted(gains, shift, mpo_count))
    left_rows = jnp.stack(left_parts).reshape(
        mpo_count, term_local * block_width, block_width
    )
    gain_rows = jnp.stack(gain_parts).reshape(mpo_count * term_local, class_count)

    mine = lax.dynamic_slice_in_dim(requests, bond_index, 1, axis=0).reshape(
        sec_local, class_count
    )
    sources = (mine // sec_local).astype(jnp.int32)
    right_parts = []
    for shift in range(mpo_count):
        target = (mpo_index + shift) % mpo_count
        picked = jnp.take(
            got_right,
            lax.dynamic_index_in_dim(sources, target, 0, keepdims=False),
            axis=0,
            mode="clip",
        )
        right_parts.append(picked if shift == 0 else shifted(picked, shift, mpo_count))
    right_rows = jnp.stack(right_parts)

    wave_rows = lax.dynamic_index_in_dim(wave_blocks, mpo_index, 0, keepdims=False)
    done = apply_blocks(gain_rows, wave_rows, left_rows, right_rows)

    out_parts = [done] + [shifted(done, shift, mpo_count) for shift in range(1, mpo_count)]
    stacked = jnp.stack(out_parts)
    order = (mpo_index - jnp.arange(mpo_count, dtype=jnp.int32)) % mpo_count
    return jnp.take(stacked, order, axis=0, mode="clip")


def solution(mesh):
    return jax.shard_map(
        per_device,
        mesh=mesh,
        in_specs=(
            P("bond", None, None, None),
            P("bond", "mpo", None),
            P("bond", "mpo", None),
            P("mpo", None),
            P("mpo", None),
            P(),
        ),
        out_specs=P("bond", None, None, None),
        check_vma=False,
    )
```

time: 167 us -> 142 us (0.85)
  waiting for transfers between devices: 107 us -> 72.4 us
  starting transfers between devices: 12.3 us -> 33.6 us
  between operations: 13.5 us -> 0.28 us
  Pallas kernels: 21.5 us -> 11.6 us
  local copies, waits for them, and re-layouts: 10.1 us -> 18.3 us
  other arithmetic: 1.96 us -> 4.14 us
    psum x1 -> x0, waiting for transfers between devices: 47.5 us -> none  [per_device(): summed = lax.psum(partial_sum, 'mpo')]
    ppermute x0 -> x12, starting transfers between devices: none -> 21.2 us  [shifted(): return lax.ppermute(value, 'mpo', pairs)]
    ppermute x0 -> x12, waiting for transfers between devices: none -> 18 us  [shifted(): return lax.ppermute(value, 'mpo', pairs)]
    gather x0 -> x5, local copies, waits for them, and re-layouts: none -> 11 us  [the longest x4 9.39 us: per_device(): jnp.take(got_right, lax.dynamic_index_in_dim(sources, target, 0, keepdims...]
    pallas_call x1, Pallas kernels: 21.5 us -> 11.6 us  [apply_blocks(): pl.pallas_call(block_kernel, out_shape=jax.ShapeDtypeStruct(wave_rows.sha...]
    all_to_all x1, waiting for transfers between devices: 59.9 us -> 54.4 us  [per_device(): lax.all_to_all(send_right, 'bond', split_axis=0, concat_axis=0, tiled=True)]
    unnamed x13 -> x12, local copies, waits for them, and re-layouts: 4.05 us -> 0.24 us
    another operation x0 -> x4, other arithmetic: none -> 3.15 us  [the longest x1 1.25 us: per_device(): right_rows = jnp.stack(right_parts)]
  transfers between devices with their start and end apart: 2 -> 13, of which waited for: 2 -> 5; matrix products, arithmetic and copies ran while one was open for 1% -> 9% of each run, Pallas kernels for 0% -> 0%
where the time goes in v4:
time: 142 us; the launch traced here: 140 us
  waiting for transfers between devices  72.4 us (51%)
  starting transfers between devices  33.6 us (24%)
  local copies, waits for them, and re-layouts  18.3 us (13%)
  Pallas kernels  11.6 us (8%)
  other arithmetic  4.14 us (3%)
    all_to_all x1, waiting for transfers between devices, per_device(): lax.all_to_all(send_right, 'bond', split_axis=0, concat_axis=0, tiled=True)  54.4 us
    ppermute x12, starting transfers between devices, shifted(): return lax.ppermute(value, 'mpo', pairs)  21.2 us
    ppermute x12, waiting for transfers between devices, shifted(): return lax.ppermute(value, 'mpo', pairs)  18 us
    all_to_all x1, starting transfers between devices, per_device(): lax.all_to_all(send_right, 'bond', split_axis=0, concat_axis=0, tiled=True)  12.4 us
    pallas_call x1, Pallas kernels, apply_blocks(): pl.pallas_call(block_kernel, out_shape=jax.ShapeDtypeStruct(wave_rows.sha...  11.6 us
    gather x4, local copies, waits for them, and re-layouts, per_device(): jnp.take(got_right, lax.dynamic_index_in_dim(sources, target, 0, keepdims...  9.39 us
  transfers between devices with their start and end apart: 13, of which 5 were waited for; matrix products, arithmetic and copies ran while one was open for 9% of the time, Pallas kernels for 0%

profile of v4, /device:TPU:8, one launch (start us, length us, event | category | flops | bytes accessed | tf_op | source)
XLA Modules:
  0.0 140.4 jit_solution(3363094581958223456)
XLA Ops:
  0.0 0.0 copy-start
  0.0 0.8 fusion.2
  0.8 0.1 reduce_sum.14
  0.9 0.1 reduce_sum.18
  1.0 1.3 reshape.73
  2.4 0.9 copy.9
  3.3 0.2 reshape.74
  3.5 2.4 %gather_fusion = bf16[64,160,128]{2,1,0:T(8,128)(2,1)} fusion(bf16[4,160,128]{2,1,0:T(8,128)(2,1)S(1)} %reshape.74, s32[1024]{0:T(1024)S(1)} %pad_clamp_fusion.5), kind=kCustom, calls=%fused_computation | custom fusion | bytes 5243136 | tf_op jit(solution)/shard_map/jit(_take)/gather | solution.py:114
  5.9 0.0 copy-start.3
  5.9 0.0 copy-start.4
  5.9 0.0 copy-start.1
  5.9 0.0 copy-start.2
  5.9 12.4 %all-to-all-start = ((bf16[64,160,128]{2,1,0:T(8,128)(2,1)}), bf16[64,160,128]{2,1,0:T(8,128)(2,1)}, u32[]{:S(2)}, u32[]{:S(2)}) async-start(bf16[64,160,128]{2,1,0:T(8,128)(2,1)} %gather_fusion), calls=%async_computation | async-start | bytes 5242880 | tf_op jit(solution)/shard_map/all_to_all | solution.py:115
  18.3 0.0 copy-done.3
  18.4 0.0 copy-done.4
  18.4 1.6 %collective-permute-start = (f32[5,8]{1,0:T(8,128)S(1)}, f32[5,8]{1,0:T(8,128)S(1)}, u32[]{:S(2)}, u32[]{:S(2)}) collective-permute-start(f32[5,8]{1,0:T(8,128)S(1)} %convert_multiply_fusion), channel_id=1, source_target_pairs={{0,1},{1,2},{2,3},{3,0},{4,5},{5,6},{6,7},{7,4},{8,9},{9,10},{10,1... | collective-permute-start | bytes 488 | tf_op jit(solution)/shard_map/ppermute | solution.py:91
  19.9 2.7 %collective-permute-start.1 = (f32[5,8]{1,0:T(8,128)S(1)}, f32[5,8]{1,0:T(8,128)S(1)}, u32[]{:S(2)}, u32[]{:S(2)}) collective-permute-start(f32[5,8]{1,0:T(8,128)S(1)} %convert_multiply_fusion), channel_id=1, source_target_pairs={{0,2},{1,3},{2,0},{3,1},{4,6},{5,7},{6,4},{7,5},{8,10},{9,11},{10,... | collective-permute-start | bytes 488 | tf_op jit(solution)/shard_map/ppermute | solution.py:91
  22.7 1.4 %collective-permute-start.2 = (f32[5,8]{1,0:T(8,128)S(1)}, f32[5,8]{1,0:T(8,128)S(1)}, u32[]{:S(2)}, u32[]{:S(2)}) collective-permute-start(f32[5,8]{1,0:T(8,128)S(1)} %convert_multiply_fusion), channel_id=1, source_target_pairs={{0,3},{1,0},{2,1},{3,2},{4,7},{5,4},{6,5},{7,6},{8,11},{9,8},{10,9... | collective-permute-start | bytes 488 | tf_op jit(solution)/shard_map/ppermute | solution.py:91
  24.1 0.0 copy-done.1
  24.1 0.1 copy.8
  24.2 0.2 reshape.72
  24.5 0.7 collective-permute-start.3
  25.1 0.0 copy-done.2
  25.1 0.1 copy.10
  25.3 0.1 reshape.75
  25.4 0.1 reshape.76
  25.6 0.0 copy-done
  25.6 0.7 dynamic-slice_bitcast_fusion.wave_ref
  26.3 54.4 %all-to-all-done = bf16[64,160,128]{2,1,0:T(8,128)(2,1)} async-done(((bf16[64,160,128]{2,1,0:T(8,128)(2,1)}), bf16[64,160,128]{2,1,0:T(8,128)(2,1)}, u32[]{:S(2)}, u32[]{:S(2)}) %all-to-all-start) | async-done | bytes 2621472 | tf_op jit(solution)/shard_map/all_to_all | solution.py:115
  80.8 2.3 %gather_fusion.2 = bf16[8,160,128]{2,1,0:T(8,128)(2,1)S(1)} fusion(bf16[64,160,128]{2,1,0:T(8,128)(2,1)} %all-to-all-done, s32[1024]{0:T(1024)S(1)} %pad_clamp_fusion.3), kind=kCustom, calls=%fused_computation.2 | custom fusion | bytes 655392 | tf_op jit(solution)/shard_map/jit(_take)/gather | solution.py:138
  83.1 1.6 %collective-permute-start.6 = (bf16[8,160,128]{2,1,0:T(8,128)(2,1)S(1)}, bf16[8,160,128]{2,1,0:T(8,128)(2,1)S(1)}, u32[]{:S(2)}, u32[]{:S(2)}) collective-permute-start(bf16[8,160,128]{2,1,0:T(8,128)(2,1)S(1)} %gather_fusion.2), channel_id=1, source_target_pairs={{0,1},{1,2},{2,3},{3,0},{4,5},{5,6},{6,7},{7,4},{8,9},{9,10},{10,1... | collective-permute-start | bytes 983048 | tf_op jit(solution)/shard_map/ppermute | solution.py:91
  84.7 2.3 %gather_fusion.3 = bf16[8,160,128]{2,1,0:T(8,128)(2,1)S(1)} fusion(bf16[64,160,128]{2,1,0:T(8,128)(2,1)} %all-to-all-done, s32[1024]{0:T(1024)S(1)} %pad_clamp_fusion.2), kind=kCustom, calls=%fused_computation.3 | custom fusion | bytes 655392 | tf_op jit(solution)/shard_map/jit(_take)/gather | solution.py:138
  87.0 2.4 %gather_fusion.4 = bf16[8,160,128]{2,1,0:T(8,128)(2,1)S(1)} fusion(bf16[64,160,128]{2,1,0:T(8,128)(2,1)} %all-to-all-done, s32[1024]{0:T(1024)S(1)} %pad_clamp_fusion.1), kind=kCustom, calls=%fused_computation.4 | custom fusion | bytes 655392 | tf_op jit(solution)/shard_map/jit(_take)/gather | solution.py:138
  89.4 0.0 collective-permute-done
  89.4 2.8 %collective-permute-start.7 = (bf16[8,160,128]{2,1,0:T(8,128)(2,1)S(1)}, bf16[8,160,128]{2,1,0:T(8,128)(2,1)S(1)}, u32[]{:S(2)}, u32[]{:S(2)}) collective-permute-start(bf16[8,160,128]{2,1,0:T(8,128)(2,1)S(1)} %gather_fusion.3), channel_id=1, source_target_pairs={{0,2},{1,3},{2,0},{3,1},{4,6},{5,7},{6,4},{7,5},{8,10},{9,11},{10,... | collective-permute-start | bytes 983048 | tf_op jit(solution)/shard_map/ppermute | solution.py:91
  92.2 0.0 collective-permute-done.1
  92.2 1.4 %collective-permute-start.8 = (bf16[8,160,128]{2,1,0:T(8,128)(2,1)S(1)}, bf16[8,160,128]{2,1,0:T(8,128)(2,1)S(1)}, u32[]{:S(2)}, u32[]{:S(2)}) collective-permute-start(bf16[8,160,128]{2,1,0:T(8,128)(2,1)S(1)} %gather_fusion.4), channel_id=1, source_target_pairs={{0,3},{1,0},{2,1},{3,2},{4,7},{5,4},{6,5},{7,6},{8,11},{9,8},{10,9... | collective-permute-start | bytes 983048 | tf_op jit(solution)/shard_map/ppermute | solution.py:91
  93.7 0.1 stack.65
  93.8 0.0 collective-permute-done.2
  93.8 0.6 collective-permute-start.4
  94.4 0.0 collective-permute-done.3
  94.4 2.8 %collective-permute-start.5 = (bf16[160,128]{1,0:T(8,128)(2,1)S(1)}, bf16[160,128]{1,0:T(8,128)(2,1)S(1)}, u32[]{:S(2)}, u32[]{:S(2)}) collective-permute-start(bf16[160,128]{1,0:T(8,128)(2,1)S(1)} %get-tuple-element.6), channel_id=1, source_target_pairs={{0,3},{1,0},{2,1},{3,2},{4,7},{5,4},{6,5},{7,6},{8,11},{9,8},{10,9... | collective-permute-start | bytes 122888 | tf_op jit(solution)/shard_map/ppermute | solution.py:91
  97.1 0.6 reshape.130.gain_ref
  97.7 0.1 stack.66
  97.8 3.3 %collective-permute-done.4 = bf16[160,128]{1,0:T(8,128)(2,1)S(1)} collective-permute-done((bf16[160,128]{1,0:T(8,128)(2,1)S(1)}, bf16[160,128]{1,0:T(8,128)(2,1)S(1)}, u32[]{:S(2)}, u32[]{:S(2)}) %collective-permute-start.4) | collective-permute-done | bytes 40992 | tf_op jit(solution)/shard_map/ppermute | solution.py:91
  101.1 0.1 stack.67
  101.2 5.2 %collective-permute-done.5 = bf16[160,128]{1,0:T(8,128)(2,1)S(1)} collective-permute-done((bf16[160,128]{1,0:T(8,128)(2,1)S(1)}, bf16[160,128]{1,0:T(8,128)(2,1)S(1)}, u32[]{:S(2)}, u32[]{:S(2)}) %collective-permute-start.5) | collective-permute-done | bytes 40992 | tf_op jit(solution)/shard_map/ppermute | solution.py:91
  106.4 0.1 stack.68
  106.5 0.8 pad_maximum_fusion.2.left_ref
  107.3 2.3 %gather_fusion.1 = bf16[8,160,128]{2,1,0:T(8,128)(2,1)S(1)} fusion(bf16[64,160,128]{2,1,0:T(8,128)(2,1)} %all-to-all-done, s32[1024]{0:T(1024)S(1)} %pad_clamp_fusion.4), kind=kCustom, calls=%fused_computation.1 | custom fusion | bytes 655392 | tf_op jit(solution)/shard_map/jit(_take)/gather | solution.py:138
  109.7 0.0 collective-permute-done.6
  109.7 0.0 collective-permute-done.7
  109.7 0.0 collective-permute-done.8
  109.7 1.3 pad_maximum_fusion.right_ref
  111.0 11.6 %shard_map.64 = bf16[8,64,256]{2,1,0:T(8,128)(2,1)} custom-call(f32[20,8]{1,0:T(8,128)} %reshape.130.gain_ref, bf16[8,64,256]{2,1,0:T(8,128)(2,1)} %dynamic-slice_bitcast_fusion.wave_ref, bf16[4,320,64]{2,1,0:T(8,128)(2,1)} %pad_maximum_fusion.2.left_ref, bf16[4,8,160,128]{3,2,1,0:T(8,128)(2,1)} %pad_maximum_fusion.right_ref), custom_call_target="tpu_custom_call" | custom-call | flops 2013265920 | bytes 1998848 | tf_op jit(solution)/shard_map/pallas_call | solution.py:73
  122.5 2.1 %collective-permute-start.9 = (bf16[8,64,256]{2,1,0:T(8,128)(2,1)}, bf16[8,64,256]{2,1,0:T(8,128)(2,1)S(1)}, u32[]{:S(2)}, u32[]{:S(2)}) collective-permute-start(bf16[8,64,256]{2,1,0:T(8,128)(2,1)} %shard_map.64), channel_id=1, source_target_pairs={{0,1},{1,2},{2,3},{3,0},{4,5},{5,6},{6,7},{7,4},{8,9},{9,10},{10,1... | collective-permute-start | bytes 786440 | tf_op jit(solution)/shard_map/ppermute | solution.py:91
  124.6 2.0 %collective-permute-start.10 = (bf16[8,64,256]{2,1,0:T(8,128)(2,1)}, bf16[8,64,256]{2,1,0:T(8,128)(2,1)S(1)}, u32[]{:S(2)}, u32[]{:S(2)}) collective-permute-start(bf16[8,64,256]{2,1,0:T(8,128)(2,1)} %shard_map.64), channel_id=1, source_target_pairs={{0,2},{1,3},{2,0},{3,1},{4,6},{5,7},{6,4},{7,5},{8,10},{9,11},{10,... | collective-permute-start | bytes 786440 | tf_op jit(solution)/shard_map/ppermute | solution.py:91
  126.6 1.6 %collective-permute-start.11 = (bf16[8,64,256]{2,1,0:T(8,128)(2,1)}, bf16[8,64,256]{2,1,0:T(8,128)(2,1)S(1)}, u32[]{:S(2)}, u32[]{:S(2)}) collective-permute-start(bf16[8,64,256]{2,1,0:T(8,128)(2,1)} %shard_map.64), channel_id=1, source_target_pairs={{0,3},{1,0},{2,1},{3,2},{4,7},{5,4},{6,5},{7,6},{8,11},{9,8},{10,9... | collective-permute-start | bytes 786440 | tf_op jit(solution)/shard_map/ppermute | solution.py:91
  128.2 3.4 %collective-permute-done.9 = bf16[8,64,256]{2,1,0:T(8,128)(2,1)S(1)} collective-permute-done((bf16[8,64,256]{2,1,0:T(8,128)(2,1)}, bf16[8,64,256]{2,1,0:T(8,128)(2,1)S(1)}, u32[]{:S(2)}, u32[]{:S(2)}) %collective-permute-start.9) | collective-permute-done | bytes 262176 | tf_op jit(solution)/shard_map/ppermute | solution.py:91
  131.6 6.0 %collective-permute-done.10 = bf16[8,64,256]{2,1,0:T(8,128)(2,1)S(1)} collective-permute-done((bf16[8,64,256]{2,1,0:T(8,128)(2,1)}, bf16[8,64,256]{2,1,0:T(8,128)(2,1)S(1)}, u32[]{:S(2)}, u32[]{:S(2)}) %collective-permute-start.10) | collective-permute-done | bytes 262176 | tf_op jit(solution)/shard_map/ppermute | solution.py:91
  137.7 0.0 collective-permute-done.11
  137.7 1.1 pad_maximum_fusion.1
  138.8 1.6 %gather_fusion.5 = bf16[4,8,64,256]{3,2,1,0:T(8,128)(2,1)} fusion(bf16[4,8,64,256]{3,2,1,0:T(8,128)(2,1)S(1)} %pad_maximum_fusion.1, s32[1024]{0:T(1024)S(1)} %pad_clamp_fusion), kind=kCustom, calls=%fused_computation.5 | custom fusion | bytes 2097168 | tf_op jit(solution)/shard_map/jit(_take)/gather | solution.py:153
  (13 shorter events, 0.1 us)
Async XLA Ops:
  0.0 25.6 %copy-start = (bf16[4,8,64,256]{3,2,1,0:T(8,128)(2,1)S(1)}, bf16[4,8,64,256]{3,2,1,0:T(8,128)(2,1)}, u32[]{:S(2)}) copy-start(bf16[4,8,64,256]{3,2,1,0:T(8,128)(2,1)} %param.6) | copy-start | bytes 3145732
  5.9 12.4 %copy-start.3 = (f32[5,8]{1,0:T(8,128)S(1)}, f32[5,8]{1,0:T(8,128)}, u32[]{:S(2)}) copy-start(f32[5,8]{1,0:T(8,128)} %param.9) | copy-start | bytes 484
  5.9 12.4 %copy-start.4 = (s32[5,8]{1,0:T(8,128)S(1)}, s32[5,8]{1,0:T(8,128)}, u32[]{:S(2)}) copy-start(s32[5,8]{1,0:T(8,128)} %param.10) | copy-start | bytes 484
  5.9 18.2 %copy-start.1 = (bf16[4,5,4096]{2,0,1:T(4,128)(2,1)S(1)}, bf16[4,5,4096]{2,0,1:T(4,128)(2,1)}, u32[]{:S(2)}) copy-start(bf16[4,5,4096]{2,0,1:T(4,128)(2,1)} %param.7) | copy-start | bytes 491524
  5.9 19.2 %copy-start.2 = (s32[256,8]{0,1:T(8,128)S(1)}, s32[256,8]{0,1:T(8,128)}, u32[]{:S(2)}) copy-start(s32[256,8]{0,1:T(8,128)} %param.11) | copy-start | bytes 24580
  5.9 74.8 %all-to-all-start = ((bf16[64,160,128]{2,1,0:T(8,128)(2,1)}), bf16[64,160,128]{2,1,0:T(8,128)(2,1)}, u32[]{:S(2)}, u32[]{:S(2)}) async-start(bf16[64,160,128]{2,1,0:T(8,128)(2,1)} %gather_fusion), calls=%async_computation | async-start | bytes 5242880 | tf_op jit(solution)/shard_map/all_to_all | solution.py:115
  18.4 71.0 %collective-permute-start = (f32[5,8]{1,0:T(8,128)S(1)}, f32[5,8]{1,0:T(8,128)S(1)}, u32[]{:S(2)}, u32[]{:S(2)}) collective-permute-start(f32[5,8]{1,0:T(8,128)S(1)} %convert_multiply_fusion), channel_id=1, source_target_pairs={{0,1},{1,2},{2,3},{3,0},{4,5},{5,6},{6,7},{7,4},{8,9},{9,10},{10,1... | collective-permute-start | bytes 488 | tf_op jit(solution)/shard_map/ppermute | solution.py:91
  19.9 72.3 %collective-permute-start.1 = (f32[5,8]{1,0:T(8,128)S(1)}, f32[5,8]{1,0:T(8,128)S(1)}, u32[]{:S(2)}, u32[]{:S(2)}) collective-permute-start(f32[5,8]{1,0:T(8,128)S(1)} %convert_multiply_fusion), channel_id=1, source_target_pairs={{0,2},{1,3},{2,0},{3,1},{4,6},{5,7},{6,4},{7,5},{8,10},{9,11},{10,... | collective-permute-start | bytes 488 | tf_op jit(solution)/shard_map/ppermute | solution.py:91
  22.7 71.1 %collective-permute-start.2 = (f32[5,8]{1,0:T(8,128)S(1)}, f32[5,8]{1,0:T(8,128)S(1)}, u32[]{:S(2)}, u32[]{:S(2)}) collective-permute-start(f32[5,8]{1,0:T(8,128)S(1)} %convert_multiply_fusion), channel_id=1, source_target_pairs={{0,3},{1,0},{2,1},{3,2},{4,7},{5,4},{6,5},{7,6},{8,11},{9,8},{10,9... | collective-permute-start | bytes 488 | tf_op jit(solution)/shard_map/ppermute | solution.py:91
  24.5 69.9 %collective-permute-start.3 = (bf16[160,128]{1,0:T(8,128)(2,1)S(1)}, bf16[160,128]{1,0:T(8,128)(2,1)S(1)}, u32[]{:S(2)}, u32[]{:S(2)}) collective-permute-start(bf16[160,128]{1,0:T(8,128)(2,1)S(1)} %get-tuple-element.8), channel_id=1, source_target_pairs={{0,1},{1,2},{2,3},{3,0},{4,5},{5,6},{6,7},{7,4},{8,9},{9,10},{10,1... | collective-permute-start | bytes 122888 | tf_op jit(solution)/shard_map/ppermute | solution.py:91
  83.1 26.6 %collective-permute-start.6 = (bf16[8,160,128]{2,1,0:T(8,128)(2,1)S(1)}, bf16[8,160,128]{2,1,0:T(8,128)(2,1)S(1)}, u32[]{:S(2)}, u32[]{:S(2)}) collective-permute-start(bf16[8,160,128]{2,1,0:T(8,128)(2,1)S(1)} %gather_fusion.2), channel_id=1, source_target_pairs={{0,1},{1,2},{2,3},{3,0},{4,5},{5,6},{6,7},{7,4},{8,9},{9,10},{10,1... | collective-permute-start | bytes 983048 | tf_op jit(solution)/shard_map/ppermute | solution.py:91
  89.4 20.3 %collective-permute-start.7 = (bf16[8,160,128]{2,1,0:T(8,128)(2,1)S(1)}, bf16[8,160,128]{2,1,0:T(8,128)(2,1)S(1)}, u32[]{:S(2)}, u32[]{:S(2)}) collective-permute-start(bf16[8,160,128]{2,1,0:T(8,128)(2,1)S(1)} %gather_fusion.3), channel_id=1, source_target_pairs={{0,2},{1,3},{2,0},{3,1},{4,6},{5,7},{6,4},{7,5},{8,10},{9,11},{10,... | collective-permute-start | bytes 983048 | tf_op jit(solution)/shard_map/ppermute | solution.py:91
  92.2 17.5 %collective-permute-start.8 = (bf16[8,160,128]{2,1,0:T(8,128)(2,1)S(1)}, bf16[8,160,128]{2,1,0:T(8,128)(2,1)S(1)}, u32[]{:S(2)}, u32[]{:S(2)}) collective-permute-start(bf16[8,160,128]{2,1,0:T(8,128)(2,1)S(1)} %gather_fusion.4), channel_id=1, source_target_pairs={{0,3},{1,0},{2,1},{3,2},{4,7},{5,4},{6,5},{7,6},{8,11},{9,8},{10,9... | collective-permute-start | bytes 983048 | tf_op jit(solution)/shard_map/ppermute | solution.py:91
  93.8 7.3 %collective-permute-start.4 = (bf16[160,128]{1,0:T(8,128)(2,1)S(1)}, bf16[160,128]{1,0:T(8,128)(2,1)S(1)}, u32[]{:S(2)}, u32[]{:S(2)}) collective-permute-start(bf16[160,128]{1,0:T(8,128)(2,1)S(1)} %get-tuple-element.7), channel_id=1, source_target_pairs={{0,2},{1,3},{2,0},{3,1},{4,6},{5,7},{6,4},{7,5},{8,10},{9,11},{10,... | collective-permute-start | bytes 122888 | tf_op jit(solution)/shard_map/ppermute | solution.py:91
  94.4 12.0 %collective-permute-start.5 = (bf16[160,128]{1,0:T(8,128)(2,1)S(1)}, bf16[160,128]{1,0:T(8,128)(2,1)S(1)}, u32[]{:S(2)}, u32[]{:S(2)}) collective-permute-start(bf16[160,128]{1,0:T(8,128)(2,1)S(1)} %get-tuple-element.6), channel_id=1, source_target_pairs={{0,3},{1,0},{2,1},{3,2},{4,7},{5,4},{6,5},{7,6},{8,11},{9,8},{10,9... | collective-permute-start | bytes 122888 | tf_op jit(solution)/shard_map/ppermute | solution.py:91
  122.5 9.1 %collective-permute-start.9 = (bf16[8,64,256]{2,1,0:T(8,128)(2,1)}, bf16[8,64,256]{2,1,0:T(8,128)(2,1)S(1)}, u32[]{:S(2)}, u32[]{:S(2)}) collective-permute-start(bf16[8,64,256]{2,1,0:T(8,128)(2,1)} %shard_map.64), channel_id=1, source_target_pairs={{0,1},{1,2},{2,3},{3,0},{4,5},{5,6},{6,7},{7,4},{8,9},{9,10},{10,1... | collective-permute-start | bytes 786440 | tf_op jit(solution)/shard_map/ppermute | solution.py:91
  124.6 13.1 %collective-permute-start.10 = (bf16[8,64,256]{2,1,0:T(8,128)(2,1)}, bf16[8,64,256]{2,1,0:T(8,128)(2,1)S(1)}, u32[]{:S(2)}, u32[]{:S(2)}) collective-permute-start(bf16[8,64,256]{2,1,0:T(8,128)(2,1)} %shard_map.64), channel_id=1, source_target_pairs={{0,2},{1,3},{2,0},{3,1},{4,6},{5,7},{6,4},{7,5},{8,10},{9,11},{10,... | collective-permute-start | bytes 786440 | tf_op jit(solution)/shard_map/ppermute | solution.py:91
  126.6 11.1 %collective-permute-start.11 = (bf16[8,64,256]{2,1,0:T(8,128)(2,1)}, bf16[8,64,256]{2,1,0:T(8,128)(2,1)S(1)}, u32[]{:S(2)}, u32[]{:S(2)}) collective-permute-start(bf16[8,64,256]{2,1,0:T(8,128)(2,1)} %shard_map.64), channel_id=1, source_target_pairs={{0,3},{1,0},{2,1},{3,2},{4,7},{5,4},{6,5},{7,6},{8,11},{9,8},{10,9... | collective-permute-start | bytes 786440 | tf_op jit(solution)/shard_map/ppermute | solution.py:91
